TPU v7x, 512 devices: a whole 4x4x16 slice. The times are simulated.
512 devices in a mesh: dp: 64 (over y, z), tensor: 8 (over x, core).
Axes of the slice: x: 4, y: 4, z: 16, core: 2. Of those that a mesh axis runs over, the one named last changes fastest.
Arguments:
- tokens: bfloat16 [65536, 1408], P(('dp', 'tensor')), may hold values from -6 to 6
- ln1_gain: float32 [1408], replicated, may hold values from 0.1 to 1.9
- ln1_shift: float32 [1408], replicated, may hold values from -3 to 3
- w_qkv: bfloat16 [1408, 16, 264], P(None, 'tensor')
- w_out: bfloat16 [16, 88, 1408], P('tensor'), may hold values from -0.625 to 0.625
- ln2_gain: float32 [1408], replicated, may hold values from 0.1 to 1.9
- ln2_shift: float32 [1408], replicated, may hold values from -3 to 3
- w_proj: bfloat16 [5632, 3584], P('dp', 'tensor'), may hold values from -0.078125 to 0.078125
- proj_bias: float32 [3584], P('tensor'), may hold values from -3 to 3
- segments: int32 [64, 256], P('dp'), may hold values from 0 to 7, never falling along the last dimension, each value on 1 to 128 neighbouring positions
- owners: int32 [16384, 1], P('dp'), may hold values from 0 to 63; in each aligned block of 256 rows (0 to 255, 256 to 511, ...) at most 8 rows name the same one
Outputs:
- delivered: bfloat16 [32768, 3584], P('dp', 'tensor')
Inputs may be any that keep to these rules, and one draw needn't show every extreme that they name: `segments`: within a pack numbers never fall, every image has 1 to 128 groups and one has exactly that many. `owners`: among the 256 merged tokens of one pack no owner gets more than 8; in some pack an owner gets exactly 8.
All inputs are finite; a program needn't handle non-finite values.
Results may differ from a plain program's by a relative error of at most 0.015.
Values may be sent and summed in bfloat16 or wider, within the bound.
No kernel may reach another device: no remote copies, remote signals or barrier semaphores. Data moves between devices by JAX's collectives and lax.ppermute only.
A program may use at most 64 MiB of HBM per device.

v0:
```python
import jax
import jax.numpy as jnp
from jax import lax
from jax.sharding import PartitionSpec as P


def layer_norm(values, gain, shift):
    wide = values.astype(jnp.float32)
    average = jnp.mean(wide, axis=-1, keepdims=True)
    centred = wide - average
    variance = jnp.mean(centred * centred, axis=-1, keepdims=True)
    return centred * lax.rsqrt(variance + 1e-06) * gain + shift


def attend(heads_qkv, token_segs):
    row_count = heads_qkv.shape[0]
    width = heads_qkv.shape[2] // 3
    queries = heads_qkv[:, :, :width]
    keys_all = heads_qkv[:, :, width : 2 * width]
    values_all = heads_qkv[:, :, 2 * width :]
    score_scale = 1.0 / jnp.sqrt(jnp.float32(width))
    block_rows = min(512, row_count)
    outputs = []
    for block_index in range(row_count // block_rows):
        lower = block_index * block_rows
        scores = (
            jnp.einsum(
                "qhd,khd->hqk",
                queries[lower : lower + block_rows],
                keys_all,
                preferred_element_type=jnp.float32,
            )
            * score_scale
        )
        same = token_segs[lower : lower + block_rows][:, None] == token_segs[None, :]
        scores = jnp.where(same[None], scores, -jnp.inf)
        row_max = jnp.max(scores, axis=-1, keepdims=True)
        exponent = jnp.exp(scores - row_max)
        probs = (exponent / jnp.sum(exponent, axis=-1, keepdims=True)).astype(jnp.bfloat16)
        context = jnp.einsum("hqk,khd->qhd", probs, values_all, preferred_element_type=jnp.float32)
        outputs.append(context.astype(jnp.bfloat16))
    return jnp.concatenate(outputs, axis=0)


def shards(
    tokens,
    ln1_gain,
    ln1_shift,
    w_qkv,
    w_out,
    ln2_gain,
    ln2_shift,
    w_proj,
    proj_bias,
    segments,
    owners,
):
    dp_count = lax.axis_size("dp")
    gathered = lax.all_gather(tokens, "tensor", axis=0, tiled=True)
    row_count = gathered.shape[0]
    normed = layer_norm(gathered, ln1_gain, ln1_shift).astype(jnp.bfloat16)
    heads_here = w_qkv.shape[1]
    heads_qkv = jnp.dot(
        normed, w_qkv.reshape(w_qkv.shape[0], -1), preferred_element_type=jnp.float32
    )
    heads_qkv = heads_qkv.astype(jnp.bfloat16).reshape(row_count, heads_here, -1)
    token_segs = jnp.repeat(segments[0], 4)
    context = attend(heads_qkv, token_segs).reshape(row_count, -1)
    out_flat = w_out.reshape(-1, w_out.shape[2])
    attn_all = lax.psum(
        jnp.dot(context, out_flat, preferred_element_type=jnp.float32).astype(jnp.bfloat16),
        "tensor",
    ).astype(jnp.float32)
    hidden = (gathered.astype(jnp.float32) + attn_all).astype(jnp.bfloat16)
    normed_all = layer_norm(hidden, ln2_gain, ln2_shift).astype(jnp.bfloat16)
    groups = row_count // 4
    merged = normed_all.reshape(groups, -1)
    summed = jnp.dot(
        merged, lax.all_gather(w_proj, "dp", axis=0, tiled=True), preferred_element_type=jnp.float32
    )
    projected = (summed + proj_bias).astype(jnp.bfloat16)
    dests = owners[:, 0]
    onehot = (dests[:, None] == jnp.arange(dp_count, dtype=jnp.int32)[None, :]).astype(jnp.int32)
    earlier = jnp.cumsum(onehot, axis=0) - onehot
    position = jnp.sum(earlier * onehot, axis=1)
    capacity = 2 * groups // dp_count
    slot_index = dests * capacity + position
    scatter_table = (
        slot_index[None, :] == jnp.arange(dp_count * capacity, dtype=jnp.int32)[:, None]
    ).astype(jnp.bfloat16)
    outgoing = jnp.dot(scatter_table, projected, preferred_element_type=jnp.float32).astype(
        jnp.bfloat16
    )
    outgoing = outgoing.reshape(dp_count, capacity, -1)
    arrived = lax.all_to_all(outgoing, "dp", split_axis=0, concat_axis=0, tiled=True)
    return arrived.reshape(dp_count * capacity, -1)


def solution(mesh):
    return jax.shard_map(
        shards,
        mesh=mesh,
        in_specs=(
            P(("dp", "tensor"), None),
            P(),
            P(),
            P(None, "tensor", None),
            P("tensor", None, None),
            P(),
            P(),
            P("dp", "tensor"),
            P("tensor"),
            P("dp", None),
            P("dp", None),
        ),
        out_specs=P("dp", "tensor"),
        check_vma=False,
    )
```

profile of v0, /device:TPU:8, one launch (start us, length us, event | category | flops | bytes accessed | tf_op | source)
XLA Modules:
  0.0 273.7 jit_solution(15908829058235544437)
XLA Ops:
  7.4 0.0 copy-start
  7.4 0.0 all-gather.3.cloned.1.call-start
  7.4 0.7 all-gather.3.cloned.1.call-update
  8.1 0.0 all-reduce.2.cloned.1.call-start
  8.1 0.7 slice_bitcast_fusion.1
  8.8 0.1 broadcast_in_dim.24
  8.9 0.1 eq.84
  9.0 0.1 broadcast_in_dim.28
  9.1 0.1 eq.89
  9.2 0.8 broadcast_in_dim.25
  10.0 0.1 eq.86
  10.1 0.7 broadcast_compare_fusion.1
  10.8 38.3 %all-gather.3.cloned.1.call-done = bf16[1024,1408]{1,0:T(8,128)(2,1)} async-done(((bf16[128,1408]{1,0:T(8,128)(2,1)}), bf16[1024,1408]{1,0:T(8,128)(2,1)}) %all-gather.3.cloned.1.call-update) | async-done | bytes 2883600 | tf_op jit(solution)/shard_map/all_gather | solution.py:59
  49.1 2.4 convert_reduce_fusion
  51.5 0.3 copy-done.1
  51.7 0.9 fusion.6
  52.6 0.0 copy-done
  52.7 0.0 copy-done.9
  52.7 0.0 copy-done.8
  52.7 3.1 %fusion.31 = bf16[1024,528]{0,1:T(8,128)(2,1)} fusion(bf16[1408,528]{0,1:T(8,128)(2,1)S(1)} %bitcast.40, bf16[1024,1408]{1,0:T(8,128)(2,1)S(1)} %copy-done.1, f32[1408]{0:T(1024)S(1)} %copy-done.8, f32[1408]{0:T(1024)S(1)} %copy-done.9, f32[1024]{0:T(1024)S(1)} %add_rsqrt_fusion.1, f32[1024]{0:T(1024)S(1)} %broadcast_multiply_fusion.1), kind=kOutput, calls=%fused_computation.42 | convolution fusion | flops 1531723776 | bytes 5471232 | tf_op jit(solution)/shard_map/dot_general | solution.py:63
  55.8 4.8 %fusion.90 = (f32[2,512]{1,0:T(2,128)S(1)}, f32[2,512,1024]{2,1,0:T(8,128)}) fusion(pred[512,1024]{1,0:T(8,128)(4,1)S(1)} %get-tuple-element.5, bf16[1024,2,264]{0,2,1:T(8,128)(2,1)} %bitcast.47), kind=kOutput, calls=%fused_computation.94 | convolution fusion | flops 188744704 | bytes 5263360 | tf_op jit(solution)/shard_map/sub | solution.py:38
  60.6 4.9 %fusion.81 = (f32[2,512]{1,0:T(2,128)S(1)}, f32[2,512,1024]{2,1,0:T(8,128)}) fusion(pred[512,1024]{1,0:T(8,128)(4,1)S(1)} %get-tuple-element.6, bf16[1024,2,264]{0,2,1:T(8,128)(2,1)} %bitcast.48), kind=kOutput, calls=%fused_computation.93 | convolution fusion | flops 188744704 | bytes 5263360 | tf_op jit(solution)/shard_map/sub | solution.py:38
  65.4 0.0 copy-done.11
  65.4 3.2 %fusion.37 = bf16[512,2,88]{0,2,1:T(8,128)(2,1)S(1)} fusion(f32[2,512,1024]{2,1,0:T(8,128)} %get-tuple-element.12, f32[2,512]{1,0:T(2,128)S(1)} %get-tuple-element.11, bf16[1024,2,264]{0,2,1:T(8,128)(2,1)S(1)} %bitcast.49), kind=kOutput, calls=%fused_computation.48 | convolution fusion | flops 186736640 | bytes 4739072 | tf_op jit(solution)/shard_map/hqk,khd->qhd/dot_general | solution.py:40
  68.6 0.3 copy-done.12
  68.9 0.9 fusion.38
  69.7 0.2 copy-done.4
  69.9 2.7 bitcast_convert_fusion
  72.6 0.0 all-reduce.2.cloned.1.call-update
  72.6 0.2 all-gather.5.cloned.1.call-start
  72.8 0.3 all-gather.5.cloned.1.call-update
  73.2 0.6 reduce-window.6
  73.8 0.2 slice_reduce_fusion
  74.0 0.1 fusion.74
  74.2 83.9 %all-reduce.2.cloned.1.call-done = bf16[1024,1408]{1,0:T(8,128)(2,1)} async-done(((bf16[1024,1408]{1,0:T(8,128)(2,1)}), bf16[1024,1408]{1,0:T(8,128)(2,1)}) %all-reduce.2.cloned.1.call-update) | async-done | bytes 2883600 | tf_op jit(solution)/shard_map/psum | solution.py:70
  158.0 3.6 %convert_reduce_fusion.1 = f32[1024]{0:T(1024)S(1)} fusion(bf16[1024,1408]{1,0:T(8,128)(2,1)} %all-reduce.2.cloned.1.call-done, bf16[1024,1408]{1,0:T(8,128)(2,1)} %all-gather.3.cloned.1.call-done), kind=kLoop, calls=%fused_computation.6 | loop fusion | flops 8649728 | bytes 5771264 | tf_op jit(solution)/shard_map/reduce_sum | solution.py:9
  161.7 0.0 copy-start.6
  161.7 0.0 copy-start.7
  161.7 0.7 copy-done.3
  162.4 1.2 fusion.10
  163.7 2.9 %fusion.13 = bf16[1024,1408]{1,0:T(8,128)(2,1)} fusion(f32[1408]{0:T(1024)S(1)} %copy-done.6, f32[1408]{0:T(1024)S(1)} %copy-done.7, f32[1024]{0:T(1024)S(1)} %add_rsqrt_fusion, f32[1024]{0:T(1024)S(1)} %broadcast_multiply_fusion, bf16[1024,1408]{1,0:T(8,128)(2,1)S(1)} %copy-done.3, bf16[1024,1408]{1,0:T(8,128)(2,1)S(1)} %copy-done.2), kind=kLoop, calls=%fused_computation.18 | loop fusion | flops 14417920 | bytes 8670208 | tf_op jit(solution)/shard_map/convert_element_type | solution.py:75
  166.5 5.7 %reshape.149 = bf16[256,5632]{1,0:T(8,128)(2,1)} reshape(bf16[1024,1408]{1,0:T(8,128)(2,1)} %fusion.13) | data formatting | bytes 5767168 | tf_op jit(solution)/shard_map/reshape | solution.py:77
  172.2 54.6 %all-gather.5.cloned.1.call-done = bf16[5632,448]{1,0:T(8,128)(2,1)} async-done(((bf16[88,448]{1,0:T(8,128)(2,1)}), bf16[5632,448]{1,0:T(8,128)(2,1)}) %all-gather.5.cloned.1.call-update) | async-done | bytes 5046288 | tf_op jit(solution)/shard_map/all_gather | solution.py:79
  226.8 0.0 copy-done.10
  226.8 5.5 %convolution_convert_fusion = bf16[512,448]{0,1:T(8,128)(2,1)S(1)} fusion(bf16[256,5632]{1,0:T(8,128)(2,1)} %reshape.149, bf16[5632,448]{1,0:T(8,128)(2,1)} %all-gather.5.cloned.1.call-done, f32[448]{0:T(512)S(1)} %copy-done.10, s32[256]{0:T(256)S(1)} %multiply_add_fusion), kind=kOutput, calls=%fused_computation.43 | convolution fusion | flops 1409875968 | bytes 8391424 | tf_op jit(solution)/shard_map/dot_general | solution.py:91
  232.2 0.2 copy.13
  232.4 32.8 %all_to_all.5 = bf16[64,8,448]{2,1,0:T(8,128)(2,1)S(1)} all-to-all(bf16[64,8,448]{2,1,0:T(8,128)(2,1)S(1)} %bitcast.41), channel_id=1, replica_groups=mesh['dp'=64,'tensor'=8] {'dp'}, dimensions={0} | all-to-all | bytes 917504 | tf_op jit(solution)/shard_map/all_to_all | solution.py:95
  265.3 1.0 copy.14
  (22 shorter events, 0.1 us)
Async XLA Ops:
  7.4 45.3 %copy-start = (bf16[1408,2,264]{0,2,1:T(8,128)(2,1)S(1)}, bf16[1408,2,264]{0,2,1:T(8,128)(2,1)}, u32[]{:S(2)}) copy-start(bf16[1408,2,264]{0,2,1:T(8,128)(2,1)} %param.14) | copy-start | bytes 4460548
  7.4 45.3 %copy-start.9 = (f32[1408]{0:T(1024)S(1)}, f32[1408]{0:T(1024)}, u32[]{:S(2)}) copy-start(f32[1408]{0:T(1024)} %param.12) | copy-start | bytes 16900
  7.4 45.3 %copy-start.8 = (f32[1408]{0:T(1024)S(1)}, f32[1408]{0:T(1024)}, u32[]{:S(2)}) copy-start(f32[1408]{0:T(1024)} %param.13) | copy-start | bytes 16900
  7.4 41.7 %all-gather.3.cloned.1.call-start = ((), (), s32[]{:S(2)}) async-start(), calls=%async_computation.1 | async-start | bytes 3244032 | tf_op jit(solution)/shard_map/all_gather | solution.py:59
  8.1 149.9 %all-reduce.2.cloned.1.call-start = ((), (), s32[]{:S(2)}) async-start(), calls=%async_computation.2 | async-start | bytes 5767168 | tf_op jit(solution)/shard_map/psum | solution.py:70
  49.1 2.7 copy-start.1
  60.6 4.9 %copy-start.11 = (bf16[1024,528]{0,1:T(8,128)(2,1)S(1)}, bf16[1024,528]{0,1:T(8,128)(2,1)}, u32[]{:S(2)}) copy-start(bf16[1024,528]{0,1:T(8,128)(2,1)} %fusion.31) | copy-start | bytes 3244036
  65.4 3.4 %copy-start.12 = (f32[2,512,1024]{2,1,0:T(8,128)S(1)}, f32[2,512,1024]{2,1,0:T(8,128)}, u32[]{:S(2)}) copy-start(f32[2,512,1024]{2,1,0:T(8,128)} %get-tuple-element.10) | copy-start | bytes 12582916
  68.9 1.0 copy-start.4
  69.9 3.3 %copy-start.5 = (s32[256,1]{0,1:T(1,128)S(1)}, s32[256,1]{0,1:T(1,128)}, u32[]{:S(2)}) copy-start(s32[256,1]{0,1:T(1,128)} %param.21) | copy-start | bytes 3076
  72.6 154.1 %all-gather.5.cloned.1.call-start = ((), (), s32[]{:S(2)}) async-start(), calls=%async_computation.3 | async-start | bytes 5857280 | tf_op jit(solution)/shard_map/all_gather | solution.py:79
  158.0 3.7 %copy-start.2 = (bf16[1024,1408]{1,0:T(8,128)(2,1)S(1)}, bf16[1024,1408]{1,0:T(8,128)(2,1)}, u32[]{:S(2)}) copy-start(bf16[1024,1408]{1,0:T(8,128)(2,1)} %all-gather.3.cloned.1.call-done) | copy-start | bytes 8650756
  158.0 4.4 %copy-start.3 = (bf16[1024,1408]{1,0:T(8,128)(2,1)S(1)}, bf16[1024,1408]{1,0:T(8,128)(2,1)}, u32[]{:S(2)}) copy-start(bf16[1024,1408]{1,0:T(8,128)(2,1)} %all-reduce.2.cloned.1.call-done) | copy-start | bytes 8650756
  161.7 2.0 copy-start.6
  161.7 2.0 copy-start.7
  166.5 60.2 %copy-start.10 = (f32[448]{0:T(512)S(1)}, f32[448]{0:T(512)}, u32[]{:S(2)}) copy-start(f32[448]{0:T(512)} %param.19) | copy-start | bytes 5380
Sparse Core Ops, SparseCore 0:
  10.3 38.6 all-gather.2
  72.7 85.2 all-reduce.1
Sparse Core Ops, SparseCore 1:
  76.0 150.7 all-gather.4
where the time goes:
time: 274 us
  waiting for transfers between devices  178 us (65%)
  blocking collectives  32.8 us (12%)
  matrix products  24.9 us (9%)
  between operations  15 us (5%)
  other arithmetic  12.5 us (5%)
  local copies, waits for them, and re-layouts  10.4 us (4%)
    psum x1, waiting for transfers between devices, shards(): lax.psum(jnp.dot(context, out_flat, preferred_element_type=jnp.float32).a...  83.9 us
    all_gather x1, waiting for transfers between devices, shards(): lax.all_gather(w_proj, 'dp', axis=0, tiled=True)  54.6 us
    all_gather x1, waiting for transfers between devices, shards(): gathered = lax.all_gather(tokens, 'tensor', axis=0, tiled=True)  38.3 us
    all_to_all x1, blocking collectives, shards(): lax.all_to_all(outgoing, 'dp', split_axis=0, concat_axis=0, tiled=True)  32.8 us
    sub x2, matrix products, attend(): exponent = jnp.exp(scores - row_max)  9.63 us
    reduce_sum x2, other arithmetic, layer_norm(): average = jnp.mean(wide, axis=-1, keepdims=True)  6.05 us
    reshape x1, local copies, waits for them, and re-layouts, shards(): merged = normed_all.reshape(groups, -1)  5.67 us
  transfers between devices with their start and end apart: 3, of which 3 were waited for; matrix products, arithmetic and copies ran while one was open for 6% of the time, Pallas kernels for 0%

commit v1 on v0

--- a/solution.py
+++ b/solution.py
@@ -56,8 +56,13 @@
     owners,
 ):
     dp_count = lax.axis_size("dp")
+    tp_count = lax.axis_size("tensor")
+    w_proj_all = lax.all_gather(w_proj, "dp", axis=0, tiled=True)
+    w_out_all = lax.all_gather(w_out, "tensor", axis=0, tiled=True)
+
     gathered = lax.all_gather(tokens, "tensor", axis=0, tiled=True)
     row_count = gathered.shape[0]
+    local_rows = tokens.shape[0]
     normed = layer_norm(gathered, ln1_gain, ln1_shift).astype(jnp.bfloat16)
     heads_here = w_qkv.shape[1]
     heads_qkv = jnp.dot(
@@ -65,19 +70,18 @@
     )
     heads_qkv = heads_qkv.astype(jnp.bfloat16).reshape(row_count, heads_here, -1)
     token_segs = jnp.repeat(segments[0], 4)
-    context = attend(heads_qkv, token_segs).reshape(row_count, -1)
-    out_flat = w_out.reshape(-1, w_out.shape[2])
-    attn_all = lax.psum(
-        jnp.dot(context, out_flat, preferred_element_type=jnp.float32).astype(jnp.bfloat16),
-        "tensor",
-    ).astype(jnp.float32)
-    hidden = (gathered.astype(jnp.float32) + attn_all).astype(jnp.bfloat16)
-    normed_all = layer_norm(hidden, ln2_gain, ln2_shift).astype(jnp.bfloat16)
-    groups = row_count // 4
-    merged = normed_all.reshape(groups, -1)
-    summed = jnp.dot(
-        merged, lax.all_gather(w_proj, "dp", axis=0, tiled=True), preferred_element_type=jnp.float32
+    context = attend(heads_qkv, token_segs).reshape(tp_count, local_rows, -1)
+    context_mine = lax.all_to_all(context, "tensor", split_axis=0, concat_axis=0, tiled=True)
+    out_heads = w_out_all.reshape(tp_count, -1, w_out_all.shape[2])
+    attn = jnp.einsum(
+        "sqd,sdo->qo", context_mine, out_heads, preferred_element_type=jnp.float32
     )
+    hidden = (tokens.astype(jnp.float32) + attn).astype(jnp.bfloat16)
+    normed_two = layer_norm(hidden, ln2_gain, ln2_shift).astype(jnp.bfloat16)
+    merged_mine = normed_two.reshape(local_rows // 4, -1)
+    merged = lax.all_gather(merged_mine, "tensor", axis=0, tiled=True)
+    groups = merged.shape[0]
+    summed = jnp.dot(merged, w_proj_all, preferred_element_type=jnp.float32)
     projected = (summed + proj_bias).astype(jnp.bfloat16)
     dests = owners[:, 0]
     onehot = (dests[:, None] == jnp.arange(dp_count, dtype=jnp.int32)[None, :]).astype(jnp.int32)

time: 274 us -> 340 us (1.24)
  waiting for transfers between devices: 178 us -> 226 us
  blocking collectives: 32.8 us -> 63.7 us
  other arithmetic: 12.5 us -> 5.21 us
  local copies, waits for them, and re-layouts: 10.4 us -> 5.09 us
    all_gather x1 -> x3, waiting for transfers between devices: 54.6 us -> 188 us  [the longest x1 147 us: shards(): w_proj_all = lax.all_gather(w_proj, 'dp', axis=0, tiled=True)]
    psum x1 -> x0, waiting for transfers between devices: 83.9 us -> none  [shards(): lax.psum(jnp.dot(context, out_flat, preferred_element_type=jnp.float32).a...]
    all_to_all x0 -> x1, blocking collectives: none -> 16 us  [shards(): lax.all_to_all(context, 'tensor', split_axis=0, concat_axis=0, tiled=True)]
    all_to_all x1, blocking collectives: 32.8 us -> 47.7 us  [shards(): lax.all_to_all(outgoing, 'dp', split_axis=0, concat_axis=0, tiled=True)]
    reshape x1 -> x2, local copies, waits for them, and re-layouts: 5.67 us -> 1.03 us  [the longest x1 0.98 us: shards(): merged_mine = normed_two.reshape(local_rows // 4, -1)]
    reduce_sum x2 -> x1, other arithmetic: 6.05 us -> 2.41 us  [layer_norm(): average = jnp.mean(wide, axis=-1, keepdims=True)]
  transfers between devices with their start and end apart: 3 -> 4, of which waited for: 3 -> 4; matrix products, arithmetic and copies ran while one was open for 6% -> 8% of each run, Pallas kernels for 0% -> 0%
where the time goes in v1:
time: 340 us
  waiting for transfers between devices  226 us (66%)
  blocking collectives  63.7 us (19%)
  matrix products  25.8 us (8%)
  between operations  13.3 us (4%)
  other arithmetic  5.21 us (2%)
  local copies, waits for them, and re-layouts  5.09 us (1%)
    all_gather x1, waiting for transfers between devices, shards(): w_proj_all = lax.all_gather(w_proj, 'dp', axis=0, tiled=True)  147 us
    all_to_all x1, blocking collectives, shards(): lax.all_to_all(outgoing, 'dp', split_axis=0, concat_axis=0, tiled=True)  47.7 us
    all_gather x1, waiting for transfers between devices, shards(): gathered = lax.all_gather(tokens, 'tensor', axis=0, tiled=True)  36.8 us
    all_gather x1, waiting for transfers between devices, shards(): merged = lax.all_gather(merged_mine, 'tensor', axis=0, tiled=True)  32.5 us
    all_to_all x1, blocking collectives, shards(): lax.all_to_all(context, 'tensor', split_axis=0, concat_axis=0, tiled=True)  16 us
    sub x2, matrix products, attend(): exponent = jnp.exp(scores - row_max)  9.62 us
    all_gather x1, waiting for transfers between devices, shards(): w_out_all = lax.all_gather(w_out, 'tensor', axis=0, tiled=True)  8.44 us
  transfers between devices with their start and end apart: 4, of which 4 were waited for; matrix products, arithmetic and copies ran while one was open for 8% of the time, Pallas kernels for 0%

profile of v1, /device:TPU:8, one launch (start us, length us, event | category | flops | bytes accessed | tf_op | source)
XLA Modules:
  0.0 339.7 jit_solution(10978495204272725188)
XLA Ops:
  6.5 0.0 copy-start
  6.5 0.0 all-gather.5.cloned.1.call-start
  6.5 0.7 all-gather.5.cloned.1.call-update
  7.3 0.0 all-gather.7.cloned.1.call-start
  7.3 0.7 all-gather.7.cloned.1.call-update
  8.0 0.0 all-gather.11.cloned.1.call-start
  8.1 0.7 all-gather.11.cloned.1.call-update
  8.7 0.0 all-gather.9.cloned.1.call-start
  8.8 0.7 slice_bitcast_fusion.1
  9.5 0.1 broadcast_in_dim.24
  9.5 0.1 eq.84
  9.7 0.1 broadcast_in_dim.28
  9.7 0.1 eq.89
  9.9 0.8 broadcast_in_dim.25
  10.6 0.1 eq.86
  10.8 0.7 broadcast_compare_fusion.1
  11.4 36.8 %all-gather.5.cloned.1.call-done = bf16[1024,1408]{1,0:T(8,128)(2,1)} async-done(((bf16[128,1408]{1,0:T(8,128)(2,1)}), bf16[1024,1408]{1,0:T(8,128)(2,1)}) %all-gather.5.cloned.1.call-update) | async-done | bytes 2883600 | tf_op jit(solution)/shard_map/all_gather | solution.py:63
  48.2 2.4 convert_reduce_fusion
  50.6 0.3 copy-done.1
  50.9 0.9 fusion.4
  51.8 0.0 copy-done
  51.8 0.0 copy-done.7
  51.8 0.0 copy-done.6
  51.8 3.1 fusion.27
  55.0 4.8 %fusion.82 = (f32[2,512]{1,0:T(2,128)S(1)}, f32[2,512,1024]{2,1,0:T(8,128)}) fusion(pred[512,1024]{1,0:T(8,128)(4,1)S(1)} %get-tuple-element.5, bf16[1024,2,264]{0,2,1:T(8,128)(2,1)} %bitcast.63), kind=kOutput, calls=%fused_computation.86 | convolution fusion | flops 188744704 | bytes 5263360 | tf_op jit(solution)/shard_map/sub | solution.py:38
  59.8 4.8 %fusion.73 = (f32[2,512]{1,0:T(2,128)S(1)}, f32[2,512,1024]{2,1,0:T(8,128)}) fusion(pred[512,1024]{1,0:T(8,128)(4,1)S(1)} %get-tuple-element.6, bf16[1024,2,264]{0,2,1:T(8,128)(2,1)} %bitcast.64), kind=kOutput, calls=%fused_computation.85 | convolution fusion | flops 188744704 | bytes 5263360 | tf_op jit(solution)/shard_map/sub | solution.py:38
  64.6 3.2 fusion.33
  67.8 0.4 copy-done.10
  68.2 0.9 fusion.34
  69.1 0.0 copy-start.4
  69.1 0.0 copy-start.5
  69.1 0.1 copy.22
  69.3 16.0 %all_to_all.10 = bf16[8,128,176]{1,2,0:T(8,128)(2,1)S(1)} all-to-all(bf16[8,128,176]{1,2,0:T(8,128)(2,1)S(1)} %copy.18), channel_id=1, replica_groups=mesh['dp'=64,'tensor'=8] {'tensor'}, dimensions={0} | all-to-all | bytes 720896 | tf_op jit(solution)/shard_map/all_to_all | solution.py:74
  85.2 8.4 %all-gather.7.cloned.1.call-done = bf16[16,88,1408]{2,1,0:T(8,128)(2,1)} async-done(((bf16[2,88,1408]{2,1,0:T(8,128)(2,1)}), bf16[16,88,1408]{2,1,0:T(8,128)(2,1)}) %all-gather.7.cloned.1.call-update) | async-done | bytes 3964944 | tf_op jit(solution)/shard_map/all_gather | solution.py:61
  93.7 3.0 fusion.91
  96.7 0.2 multiply_reduce_fusion
  96.9 0.2 add_convert_fusion
  97.1 1.0 reshape.155
  98.1 0.0 all-gather.9.cloned.1.call-update
  98.2 0.6 reduce-window.6
  98.8 0.2 slice_reduce_fusion
  99.0 0.1 fusion.67
  99.1 146.7 %all-gather.11.cloned.1.call-done = bf16[5632,448]{1,0:T(8,128)(2,1)} async-done(((bf16[88,448]{1,0:T(8,128)(2,1)}), bf16[5632,448]{1,0:T(8,128)(2,1)}) %all-gather.11.cloned.1.call-update) | async-done | bytes 5046288 | tf_op jit(solution)/shard_map/all_gather | solution.py:60
  245.8 32.5 %all-gather.9.cloned.1.call-done = bf16[256,5632]{1,0:T(8,128)(2,1)} async-done(((bf16[32,5632]{1,0:T(8,128)(2,1)}), bf16[256,5632]{1,0:T(8,128)(2,1)}) %all-gather.9.cloned.1.call-update) | async-done | bytes 2883600 | tf_op jit(solution)/shard_map/all_gather | solution.py:82
  278.3 6.0 %convolution_convert_fusion = bf16[512,448]{0,1:T(8,128)(2,1)S(1)} fusion(bf16[256,5632]{1,0:T(8,128)(2,1)} %all-gather.9.cloned.1.call-done, bf16[5632,448]{1,0:T(8,128)(2,1)} %all-gather.11.cloned.1.call-done, s32[256]{0:T(256)S(1)} %multiply_add_fusion, f32[448]{0:T(512)S(1)} %copy-done.8), kind=kOutput, calls=%fused_computation.36 | convolution fusion | flops 1409875968 | bytes 8391424 | tf_op jit(solution)/shard_map/dot_general | solution.py:95
  284.3 0.2 copy.19
  284.5 47.7 %all_to_all.11 = bf16[64,8,448]{2,1,0:T(8,128)(2,1)S(1)} all-to-all(bf16[64,8,448]{2,1,0:T(8,128)(2,1)S(1)} %bitcast.55), channel_id=1, replica_groups=mesh['dp'=64,'tensor'=8] {'dp'}, dimensions={0} | all-to-all | bytes 917504 | tf_op jit(solution)/shard_map/all_to_all | solution.py:99
  332.2 1.0 copy.20
  (24 shorter events, 0.2 us)
Async XLA Ops:
  6.5 45.3 %copy-start = (bf16[1408,2,264]{0,2,1:T(8,128)(2,1)S(1)}, bf16[1408,2,264]{0,2,1:T(8,128)(2,1)}, u32[]{:S(2)}) copy-start(bf16[1408,2,264]{0,2,1:T(8,128)(2,1)} %param.14) | copy-start | bytes 4460548
  6.5 45.3 %copy-start.7 = (f32[1408]{0:T(1024)S(1)}, f32[1408]{0:T(1024)}, u32[]{:S(2)}) copy-start(f32[1408]{0:T(1024)} %param.12) | copy-start | bytes 16900
  6.5 45.3 %copy-start.6 = (f32[1408]{0:T(1024)S(1)}, f32[1408]{0:T(1024)}, u32[]{:S(2)}) copy-start(f32[1408]{0:T(1024)} %param.13) | copy-start | bytes 16900
  6.5 41.7 %all-gather.5.cloned.1.call-start = ((), (), s32[]{:S(2)}) async-start(), calls=%async_computation.2 | async-start | bytes 3244032 | tf_op jit(solution)/shard_map/all_gather | solution.py:63
  7.3 86.4 %all-gather.7.cloned.1.call-start = ((), (), s32[]{:S(2)}) async-start(), calls=%async_computation.3 | async-start | bytes 4460544 | tf_op jit(solution)/shard_map/all_gather | solution.py:61
  8.0 237.8 %all-gather.11.cloned.1.call-start = ((), (), s32[]{:S(2)}) async-start(), calls=%async_computation.5 | async-start | bytes 5857280 | tf_op jit(solution)/shard_map/all_gather | solution.py:60
  8.7 269.5 %all-gather.9.cloned.1.call-start = ((), (), s32[]{:S(2)}) async-start(), calls=%async_computation.4 | async-start | bytes 3244032 | tf_op jit(solution)/shard_map/all_gather | solution.py:82
  48.2 2.7 copy-start.1
  59.8 4.8 %copy-start.9 = (bf16[1024,528]{0,1:T(8,128)(2,1)S(1)}, bf16[1024,528]{0,1:T(8,128)(2,1)}, u32[]{:S(2)}) copy-start(bf16[1024,528]{0,1:T(8,128)(2,1)} %fusion.27) | copy-start | bytes 3244036
  64.6 3.6 %copy-start.10 = (f32[2,512,1024]{2,1,0:T(8,128)S(1)}, f32[2,512,1024]{2,1,0:T(8,128)}, u32[]{:S(2)}) copy-start(f32[2,512,1024]{2,1,0:T(8,128)} %get-tuple-element.10) | copy-start | bytes 12582916
  68.2 25.5 %copy-start.2 = (bf16[128,1408]{1,0:T(8,128)(2,1)S(1)}, bf16[128,1408]{1,0:T(8,128)(2,1)}, u32[]{:S(2)}) copy-start(bf16[128,1408]{1,0:T(8,128)(2,1)} %param.11) | copy-start | bytes 1081348
  69.1 27.8 %copy-start.4 = (f32[1408]{0:T(1024)S(1)}, f32[1408]{0:T(1024)}, u32[]{:S(2)}) copy-start(f32[1408]{0:T(1024)} %param.17) | copy-start | bytes 16900
  69.1 27.8 %copy-start.5 = (f32[1408]{0:T(1024)S(1)}, f32[1408]{0:T(1024)}, u32[]{:S(2)}) copy-start(f32[1408]{0:T(1024)} %param.16) | copy-start | bytes 16900
  85.2 12.9 %copy-start.3 = (s32[256,1]{0,1:T(1,128)S(1)}, s32[256,1]{0,1:T(1,128)}, u32[]{:S(2)}) copy-start(s32[256,1]{0,1:T(1,128)} %param.21) | copy-start | bytes 3076
  93.7 184.6 %copy-start.8 = (f32[448]{0:T(512)S(1)}, f32[448]{0:T(512)}, u32[]{:S(2)}) copy-start(f32[448]{0:T(512)} %param.19) | copy-start | bytes 5380
Sparse Core Ops, SparseCore 0:
  9.5 38.6 all-gather.4
  50.3 43.2 all-gather.6
  96.6 149.1 all-gather.10
  247.8 30.4 all-gather.8

commit v2 on v0

--- a/solution.py
+++ b/solution.py
@@ -1,7 +1,10 @@
 import jax
 import jax.numpy as jnp
 from jax import lax
-from jax.sharding import PartitionSpec as P
+from jax.sharding import Mesh, PartitionSpec as P
+
+DP = ("y", "z")
+TP = ("x", "core")
 
 
 def layer_norm(values, gain, shift):
@@ -55,8 +58,11 @@
     segments,
     owners,
 ):
-    dp_count = lax.axis_size("dp")
-    gathered = lax.all_gather(tokens, "tensor", axis=0, tiled=True)
+    dp_count = (lax.axis_size("y") * lax.axis_size("z"))
+    ny, nz = lax.axis_size("y"), lax.axis_size("z")
+    w_zy = lax.all_gather(lax.all_gather(w_proj, "y", axis=0, tiled=True), "z", axis=0, tiled=True)
+    w_proj_all = w_zy.reshape(nz, ny, -1, w_zy.shape[1]).transpose(1, 0, 2, 3).reshape(w_zy.shape)
+    gathered = lax.all_gather(tokens, TP, axis=0, tiled=True)
     row_count = gathered.shape[0]
     normed = layer_norm(gathered, ln1_gain, ln1_shift).astype(jnp.bfloat16)
     heads_here = w_qkv.shape[1]
@@ -69,14 +75,14 @@
     out_flat = w_out.reshape(-1, w_out.shape[2])
     attn_all = lax.psum(
         jnp.dot(context, out_flat, preferred_element_type=jnp.float32).astype(jnp.bfloat16),
-        "tensor",
+        TP,
     ).astype(jnp.float32)
     hidden = (gathered.astype(jnp.float32) + attn_all).astype(jnp.bfloat16)
     normed_all = layer_norm(hidden, ln2_gain, ln2_shift).astype(jnp.bfloat16)
     groups = row_count // 4
     merged = normed_all.reshape(groups, -1)
     summed = jnp.dot(
-        merged, lax.all_gather(w_proj, "dp", axis=0, tiled=True), preferred_element_type=jnp.float32
+        merged, w_proj_all, preferred_element_type=jnp.float32
     )
     projected = (summed + proj_bias).astype(jnp.bfloat16)
     dests = owners[:, 0]
@@ -92,27 +98,27 @@
         jnp.bfloat16
     )
     outgoing = outgoing.reshape(dp_count, capacity, -1)
-    arrived = lax.all_to_all(outgoing, "dp", split_axis=0, concat_axis=0, tiled=True)
+    arrived = lax.all_to_all(outgoing, DP, split_axis=0, concat_axis=0, tiled=True)
     return arrived.reshape(dp_count * capacity, -1)
 
 
 def solution(mesh):
     return jax.shard_map(
         shards,
-        mesh=mesh,
+        mesh=Mesh(mesh.devices.reshape(4, 16, 4, 2), ("y", "z", "x", "core")),
         in_specs=(
-            P(("dp", "tensor"), None),
+            P(DP + TP, None),
             P(),
             P(),
-            P(None, "tensor", None),
-            P("tensor", None, None),
+            P(None, TP, None),
+            P(TP, None, None),
             P(),
             P(),
-            P("dp", "tensor"),
-            P("tensor"),
-            P("dp", None),
-            P("dp", None),
+            P(DP, TP),
+            P(TP),
+            P(DP, None),
+            P(DP, None),
         ),
-        out_specs=P("dp", "tensor"),
+        out_specs=P(DP, TP),
         check_vma=False,
     )

time: 274 us -> 248 us (0.905)
  the two profiles are of different devices: /device:TPU:8 before, /device:TPU:7 now
where the time goes in v2:
time: 248 us; the launch traced here: 247 us
  waiting for transfers between devices  112 us (45%)
  blocking collectives  57.1 us (23%)
  matrix products  25.3 us (10%)
  local copies, waits for them, and re-layouts  25.2 us (10%)
  between operations  15 us (6%)
  other arithmetic  12.5 us (5%)
    psum x1, waiting for transfers between devices, shards(): lax.psum(jnp.dot(context, out_flat, preferred_element_type=jnp.float32).a...  73.4 us
    all_to_all x1, blocking collectives, shards(): lax.all_to_all(outgoing, DP, split_axis=0, concat_axis=0, tiled=True)  46.3 us
    all_gather x1, waiting for transfers between devices, shards(): gathered = lax.all_gather(tokens, TP, axis=0, tiled=True)  37.9 us
    all_gather x1, blocking collectives, shards(): lax.all_gather(w_proj, 'y', axis=0, tiled=True)  10.8 us
    sub x2, matrix products, attend(): exponent = jnp.exp(scores - row_max)  9.42 us
    all_gather x1, local copies, waits for them, and re-layouts, shards(): lax.all_gather(lax.all_gather(w_proj, 'y', axis=0, tiled=True), 'z', axis...  8.19 us
    reduce_sum x2, other arithmetic, layer_norm(): average = jnp.mean(wide, axis=-1, keepdims=True)  6.1 us
    dot_general x1, matrix products, shards(): jnp.dot(scatter_table, projected, preferred_element_type=jnp.float32)  5.99 us
  transfers between devices with their start and end apart: 3, of which 2 were waited for; matrix products, arithmetic and copies ran while one was open for 7% of the time, Pallas kernels for 0%

profile of v2, /device:TPU:7, one launch (start us, length us, event | category | flops | bytes accessed | tf_op | source)
XLA Modules:
  0.0 247.3 jit_solution(11472693778949749928)
XLA Ops:
  7.4 0.0 copy-start
  7.4 0.0 all-gather.4.cloned.1.call-start
  7.4 0.7 all-gather.4.cloned.1.call-update
  8.1 0.0 all-reduce.2.cloned.1.call-start
  8.1 0.8 broadcast_in_dim.25
  8.9 0.1 eq.86
  9.0 0.7 slice_bitcast_fusion.1
  9.7 0.1 broadcast_in_dim.24
  9.8 0.1 eq.84
  9.9 0.1 broadcast_in_dim.28
  10.0 0.1 eq.89
  10.1 0.7 broadcast_compare_fusion.1
  10.8 37.9 %all-gather.4.cloned.1.call-done = bf16[1024,1408]{1,0:T(8,128)(2,1)} async-done(((bf16[128,1408]{1,0:T(8,128)(2,1)}), bf16[1024,1408]{1,0:T(8,128)(2,1)}) %all-gather.4.cloned.1.call-update) | async-done | bytes 2883600 | tf_op jit(solution)/shard_map/all_gather | solution.py:65
  48.7 2.4 convert_reduce_fusion
  51.1 0.3 copy-done.1
  51.4 0.9 fusion.6
  52.3 0.0 copy-done
  52.3 3.2 %fusion.31 = bf16[1024,528]{0,1:T(8,128)(2,1)} fusion(bf16[1408,528]{0,1:T(8,128)(2,1)S(1)} %bitcast.45, bf16[1024,1408]{1,0:T(8,128)(2,1)S(1)} %copy-done.1, f32[1408]{0:T(1024)S(1)} %copy-done.9, f32[1408]{0:T(1024)S(1)} %copy-done.10, f32[1024]{0:T(1024)S(1)} %add_rsqrt_fusion.1, f32[1024]{0:T(1024)S(1)} %broadcast_multiply_fusion.1), kind=kOutput, calls=%fused_computation.42 | convolution fusion | flops 1531723776 | bytes 5471232 | tf_op jit(solution)/shard_map/dot_general | solution.py:69
  55.5 4.6 %fusion.81 = (f32[2,512]{1,0:T(2,128)S(1)}, f32[2,512,1024]{2,1,0:T(8,128)}) fusion(pred[512,1024]{1,0:T(8,128)(4,1)S(1)} %get-tuple-element.6, bf16[1024,2,264]{0,2,1:T(8,128)(2,1)} %bitcast.55), kind=kOutput, calls=%fused_computation.93 | convolution fusion | flops 188744704 | bytes 5263360 | tf_op jit(solution)/shard_map/sub | solution.py:41
  60.2 4.8 %fusion.90 = (f32[2,512]{1,0:T(2,128)S(1)}, f32[2,512,1024]{2,1,0:T(8,128)}) fusion(pred[512,1024]{1,0:T(8,128)(4,1)S(1)} %get-tuple-element.5, bf16[1024,2,264]{0,2,1:T(8,128)(2,1)} %bitcast.56), kind=kOutput, calls=%fused_computation.94 | convolution fusion | flops 188744704 | bytes 5263360 | tf_op jit(solution)/shard_map/sub | solution.py:41
  64.9 0.0 copy-done.12
  64.9 3.2 %fusion.38 = bf16[512,2,88]{0,2,1:T(8,128)(2,1)S(1)} fusion(f32[2,512,1024]{2,1,0:T(8,128)} %get-tuple-element.10, f32[2,512]{1,0:T(2,128)S(1)} %get-tuple-element.9, bf16[1024,2,264]{0,2,1:T(8,128)(2,1)S(1)} %bitcast.57), kind=kOutput, calls=%fused_computation.49 | convolution fusion | flops 186736640 | bytes 4739072 | tf_op jit(solution)/shard_map/hqk,khd->qhd/dot_general | solution.py:43
  68.1 0.3 copy-done.13
  68.4 0.9 fusion.37
  69.2 0.2 copy-done.4
  69.4 2.6 %bitcast_convert_fusion = bf16[1024,1408]{1,0:T(8,128)(2,1)} fusion(bf16[2,88,1408]{2,1,0:T(8,128)(2,1)S(1)} %copy-done.4, bf16[512,2,88]{0,2,1:T(8,128)(2,1)S(1)} %fusion.38, bf16[512,2,88]{0,2,1:T(8,128)(2,1)S(1)} %fusion.37), kind=kOutput, calls=%fused_computation.20 | convolution fusion | flops 509673472 | bytes 3739648 | tf_op jit(solution)/shard_map/dot_general | solution.py:77
  72.1 0.0 all-reduce.2.cloned.1.call-update
  72.1 0.0 all-gather.6.cloned.1.call-start
  72.1 10.8 %all_gather.10 = bf16[352,448]{1,0:T(8,128)(2,1)S(1)} all-gather(bf16[88,448]{1,0:T(8,128)(2,1)S(1)} %copy-done.5), channel_id=1, replica_groups=mesh['y'=4,'z'=16,'x'=4,'core'=2] {'y'}, dimensions={0}, use_global_device_ids=true | all-gather | bytes 394240 | tf_op jit(solution)/shard_map/all_gather | solution.py:63
  83.0 0.9 copy.28
  83.9 0.0 all-gather.6.cloned.1.call-update
  83.9 0.6 reduce-window.6
  84.5 0.2 slice_reduce_fusion
  84.8 0.1 fusion.74
  84.9 73.4 %all-reduce.2.cloned.1.call-done = bf16[1024,1408]{1,0:T(8,128)(2,1)} async-done(((bf16[1024,1408]{1,0:T(8,128)(2,1)}), bf16[1024,1408]{1,0:T(8,128)(2,1)}) %all-reduce.2.cloned.1.call-update) | async-done | bytes 2883600 | tf_op jit(solution)/shard_map/psum | solution.py:76
  158.3 3.7 %convert_reduce_fusion.1 = f32[1024]{0:T(1024)S(1)} fusion(bf16[1024,1408]{1,0:T(8,128)(2,1)} %all-reduce.2.cloned.1.call-done, bf16[1024,1408]{1,0:T(8,128)(2,1)} %all-gather.4.cloned.1.call-done), kind=kLoop, calls=%fused_computation.6 | loop fusion | flops 8649728 | bytes 5771264 | tf_op jit(solution)/shard_map/reduce_sum | solution.py:12
  162.0 0.0 copy-start.7
  162.0 0.0 copy-start.8
  162.0 0.7 copy-done.3
  162.7 1.2 fusion.10
  164.0 2.9 %fusion.13 = bf16[1024,1408]{1,0:T(8,128)(2,1)} fusion(f32[1408]{0:T(1024)S(1)} %copy-done.7, f32[1408]{0:T(1024)S(1)} %copy-done.8, f32[1024]{0:T(1024)S(1)} %add_rsqrt_fusion, f32[1024]{0:T(1024)S(1)} %broadcast_multiply_fusion, bf16[1024,1408]{1,0:T(8,128)(2,1)S(1)} %copy-done.3, bf16[1024,1408]{1,0:T(8,128)(2,1)S(1)} %copy-done.2), kind=kLoop, calls=%fused_computation.18 | loop fusion | flops 14417920 | bytes 8670208 | tf_op jit(solution)/shard_map/convert_element_type | solution.py:81
  166.8 5.6 %reshape.155 = bf16[256,5632]{1,0:T(8,128)(2,1)} reshape(bf16[1024,1408]{1,0:T(8,128)(2,1)} %fusion.13) | data formatting | bytes 5767168 | tf_op jit(solution)/shard_map/reshape | solution.py:83
  172.4 8.2 %copy.29 = bf16[16,352,448]{2,1,0:T(8,128)(2,1)} copy(bf16[16,352,448]{1,2,0:T(8,128)(2,1)} %all-gather.6.cloned.1.call-done) | data formatting | bytes 10092544 | tf_op jit(solution)/shard_map/all_gather | solution.py:63
  180.6 5.8 %copy.30 = bf16[4,16,88,448]{3,2,1,0:T(8,128)(2,1)} copy(bf16[4,16,88,448]{3,2,0,1:T(8,128)(2,1)} %bitcast.46) | data formatting | bytes 10092544 | tf_op jit(solution)/shard_map/transpose | solution.py:64
  186.4 6.0 %convolution_convert_fusion = bf16[512,448]{0,1:T(8,128)(2,1)S(1)} fusion(bf16[256,5632]{1,0:T(8,128)(2,1)} %reshape.155, bf16[5632,448]{1,0:T(8,128)(2,1)} %bitcast.47, s32[256]{0:T(256)S(1)} %multiply_add_fusion, f32[448]{0:T(512)S(1)} %copy-done.11), kind=kOutput, calls=%fused_computation.43 | convolution fusion | flops 1409875968 | bytes 8391424 | tf_op jit(solution)/shard_map/dot_general | solution.py:97
  192.4 0.2 copy.31
  192.6 46.3 %all_to_all.5 = bf16[64,8,448]{2,1,0:T(8,128)(2,1)S(1)} all-to-all(bf16[64,8,448]{2,1,0:T(8,128)(2,1)S(1)} %bitcast.48), channel_id=1, replica_groups=mesh['y'=4,'z'=16,'x'=4,'core'=2] {'y','z'}, dimensions={0} | all-to-all | bytes 917504 | tf_op jit(solution)/shard_map/all_to_all | solution.py:101
  238.9 1.0 copy.32
  (28 shorter events, 0.1 us)
Async XLA Ops:
  7.4 44.9 %copy-start = (bf16[1408,2,264]{0,2,1:T(8,128)(2,1)S(1)}, bf16[1408,2,264]{0,2,1:T(8,128)(2,1)}, u32[]{:S(2)}) copy-start(bf16[1408,2,264]{0,2,1:T(8,128)(2,1)} %param.14) | copy-start | bytes 4460548
  7.4 44.9 %copy-start.9 = (f32[1408]{0:T(1024)S(1)}, f32[1408]{0:T(1024)}, u32[]{:S(2)}) copy-start(f32[1408]{0:T(1024)} %param.13) | copy-start | bytes 16900
  7.4 44.9 %copy-start.10 = (f32[1408]{0:T(1024)S(1)}, f32[1408]{0:T(1024)}, u32[]{:S(2)}) copy-start(f32[1408]{0:T(1024)} %param.12) | copy-start | bytes 16900
  7.4 41.3 %all-gather.4.cloned.1.call-start = ((), (), s32[]{:S(2)}) async-start(), calls=%async_computation.1 | async-start | bytes 3244032 | tf_op jit(solution)/shard_map/all_gather | solution.py:65
  8.1 150.2 %all-reduce.2.cloned.1.call-start = ((), (), s32[]{:S(2)}) async-start(), calls=%async_computation.2 | async-start | bytes 5767168 | tf_op jit(solution)/shard_map/psum | solution.py:76
  48.7 2.7 %copy-start.1 = (bf16[1024,1408]{1,0:T(8,128)(2,1)S(1)}, bf16[1024,1408]{1,0:T(8,128)(2,1)}, u32[]{:S(2)}) copy-start(bf16[1024,1408]{1,0:T(8,128)(2,1)} %all-gather.4.cloned.1.call-done) | copy-start | bytes 8650756
  60.1 4.8 %copy-start.12 = (bf16[1024,528]{0,1:T(8,128)(2,1)S(1)}, bf16[1024,528]{0,1:T(8,128)(2,1)}, u32[]{:S(2)}) copy-start(bf16[1024,528]{0,1:T(8,128)(2,1)} %fusion.31) | copy-start | bytes 3244036
  64.9 3.4 %copy-start.13 = (f32[2,512,1024]{2,1,0:T(8,128)S(1)}, f32[2,512,1024]{2,1,0:T(8,128)}, u32[]{:S(2)}) copy-start(f32[2,512,1024]{2,1,0:T(8,128)} %get-tuple-element.12) | copy-start | bytes 12582916
  68.4 1.0 copy-start.4
  69.4 2.7 %copy-start.5 = (bf16[88,448]{1,0:T(8,128)(2,1)S(1)}, bf16[88,448]{1,0:T(8,128)(2,1)}, u32[]{:S(2)}) copy-start(bf16[88,448]{1,0:T(8,128)(2,1)} %param.18) | copy-start | bytes 236548
  69.4 14.5 %copy-start.6 = (s32[256,1]{0,1:T(1,128)S(1)}, s32[256,1]{0,1:T(1,128)}, u32[]{:S(2)}) copy-start(s32[256,1]{0,1:T(1,128)} %param.21) | copy-start | bytes 3076
  72.1 100.4 %all-gather.6.cloned.1.call-start = ((), (), s32[]{:S(2)}) async-start(), calls=%async_computation.3 | async-start | bytes 5849088 | tf_op jit(solution)/shard_map/all_gather | solution.py:63
  158.3 3.7 %copy-start.2 = (bf16[1024,1408]{1,0:T(8,128)(2,1)S(1)}, bf16[1024,1408]{1,0:T(8,128)(2,1)}, u32[]{:S(2)}) copy-start(bf16[1024,1408]{1,0:T(8,128)(2,1)} %all-gather.4.cloned.1.call-done) | copy-start | bytes 8650756
  158.3 4.4 %copy-start.3 = (bf16[1024,1408]{1,0:T(8,128)(2,1)S(1)}, bf16[1024,1408]{1,0:T(8,128)(2,1)}, u32[]{:S(2)}) copy-start(bf16[1024,1408]{1,0:T(8,128)(2,1)} %all-reduce.2.cloned.1.call-done) | copy-start | bytes 8650756
  162.0 2.0 copy-start.7
  162.0 2.0 copy-start.8
  180.6 5.8 %copy-start.11 = (f32[448]{0:T(512)S(1)}, f32[448]{0:T(512)}, u32[]{:S(2)}) copy-start(f32[448]{0:T(512)} %param.19) | copy-start | bytes 5380
Sparse Core Ops, SparseCore 0:
  10.3 38.3 all-gather.3
  72.2 86.0 all-reduce.1
Sparse Core Ops, SparseCore 1:
  84.0 79.0 all-gather.5

commit v3 on v2

--- a/solution.py
+++ b/solution.py
@@ -60,8 +60,8 @@
 ):
     dp_count = (lax.axis_size("y") * lax.axis_size("z"))
     ny, nz = lax.axis_size("y"), lax.axis_size("z")
-    w_zy = lax.all_gather(lax.all_gather(w_proj, "y", axis=0, tiled=True), "z", axis=0, tiled=True)
-    w_proj_all = w_zy.reshape(nz, ny, -1, w_zy.shape[1]).transpose(1, 0, 2, 3).reshape(w_zy.shape)
+    w_y = lax.all_gather(w_proj, "y", axis=0)
+    w_proj_all = lax.all_gather(w_y, "z", axis=1).reshape(-1, w_proj.shape[1])
     gathered = lax.all_gather(tokens, TP, axis=0, tiled=True)
     row_count = gathered.shape[0]
     normed = layer_norm(gathered, ln1_gain, ln1_shift).astype(jnp.bfloat16)

time: 248 us -> 233 us (0.940)
  the two profiles are of different devices: /device:TPU:7 before, /device:TPU:15 now
where the time goes in v3:
time: 233 us
  waiting for transfers between devices  113 us (48%)
  blocking collectives  57.3 us (25%)
  matrix products  24.9 us (11%)
  between operations  15 us (6%)
  other arithmetic  12.5 us (5%)
  local copies, waits for them, and re-layouts  10.4 us (4%)
    psum x1, waiting for transfers between devices, shards(): lax.psum(jnp.dot(context, out_flat, preferred_element_type=jnp.float32).a...  74.2 us
    all_to_all x1, blocking collectives, shards(): lax.all_to_all(outgoing, DP, split_axis=0, concat_axis=0, tiled=True)  46.7 us
    all_gather x1, waiting for transfers between devices, shards(): gathered = lax.all_gather(tokens, TP, axis=0, tiled=True)  37.8 us
    all_gather x1, blocking collectives, shards(): w_y = lax.all_gather(w_proj, 'y', axis=0)  10.5 us
    sub x2, matrix products, attend(): exponent = jnp.exp(scores - row_max)  9.63 us
    reduce_sum x2, other arithmetic, layer_norm(): average = jnp.mean(wide, axis=-1, keepdims=True)  6.11 us
    reshape x1, local copies, waits for them, and re-layouts, shards(): merged = normed_all.reshape(groups, -1)  5.64 us
    dot_general x1, matrix products, shards(): jnp.dot(scatter_table, projected, preferred_element_type=jnp.float32)  5.46 us
  transfers between devices with their start and end apart: 3, of which 2 were waited for; matrix products, arithmetic and copies ran while one was open for 7% of the time, Pallas kernels for 0%

profile of v3, /device:TPU:15, one launch (start us, length us, event | category | flops | bytes accessed | tf_op | source)
XLA Modules:
  0.0 233.0 jit_solution(16947711672274592112)
XLA Ops:
  7.4 0.0 copy-start
  7.4 0.0 all-gather.5.cloned.1.call-start
  7.4 0.7 all-gather.5.cloned.1.call-update
  8.1 0.0 all-reduce.2.cloned.1.call-start
  8.1 0.7 slice_bitcast_fusion.1
  8.8 0.1 broadcast_in_dim.24
  8.9 0.1 eq.84
  9.0 0.1 broadcast_in_dim.28
  9.1 0.1 eq.89
  9.2 0.8 broadcast_in_dim.25
  10.0 0.1 eq.86
  10.1 0.7 broadcast_compare_fusion.1
  10.8 37.8 %all-gather.5.cloned.1.call-done = bf16[1024,1408]{1,0:T(8,128)(2,1)} async-done(((bf16[128,1408]{1,0:T(8,128)(2,1)}), bf16[1024,1408]{1,0:T(8,128)(2,1)}) %all-gather.5.cloned.1.call-update) | async-done | bytes 2883600 | tf_op jit(solution)/shard_map/all_gather | solution.py:65
  48.6 2.4 %convert_reduce_fusion = f32[1024]{0:T(1024)S(1)} fusion(bf16[1024,1408]{1,0:T(8,128)(2,1)} %all-gather.5.cloned.1.call-done), kind=kLoop, calls=%fused_computation.4 | loop fusion | flops 2882560 | bytes 2887680 | tf_op jit(solution)/shard_map/reduce_sum | solution.py:12
  51.0 0.3 copy-done.1
  51.3 0.9 fusion.6
  52.2 0.0 copy-done
  52.2 0.0 copy-done.10
  52.2 0.0 copy-done.9
  52.2 3.1 %fusion.31 = bf16[1024,528]{0,1:T(8,128)(2,1)} fusion(bf16[1408,528]{0,1:T(8,128)(2,1)S(1)} %bitcast.42, bf16[1024,1408]{1,0:T(8,128)(2,1)S(1)} %copy-done.1, f32[1408]{0:T(1024)S(1)} %copy-done.9, f32[1408]{0:T(1024)S(1)} %copy-done.10, f32[1024]{0:T(1024)S(1)} %add_rsqrt_fusion.1, f32[1024]{0:T(1024)S(1)} %broadcast_multiply_fusion.1), kind=kOutput, calls=%fused_computation.42 | convolution fusion | flops 1531723776 | bytes 5471232 | tf_op jit(solution)/shard_map/dot_general | solution.py:69
  55.3 4.8 %fusion.90 = (f32[2,512]{1,0:T(2,128)S(1)}, f32[2,512,1024]{2,1,0:T(8,128)}) fusion(pred[512,1024]{1,0:T(8,128)(4,1)S(1)} %get-tuple-element.5, bf16[1024,2,264]{0,2,1:T(8,128)(2,1)} %bitcast.51), kind=kOutput, calls=%fused_computation.94 | convolution fusion | flops 188744704 | bytes 5263360 | tf_op jit(solution)/shard_map/sub | solution.py:41
  60.1 4.9 %fusion.81 = (f32[2,512]{1,0:T(2,128)S(1)}, f32[2,512,1024]{2,1,0:T(8,128)}) fusion(pred[512,1024]{1,0:T(8,128)(4,1)S(1)} %get-tuple-element.6, bf16[1024,2,264]{0,2,1:T(8,128)(2,1)} %bitcast.52), kind=kOutput, calls=%fused_computation.93 | convolution fusion | flops 188744704 | bytes 5263360 | tf_op jit(solution)/shard_map/sub | solution.py:41
  65.0 0.0 copy-done.12
  65.0 3.2 %fusion.37 = bf16[512,2,88]{0,2,1:T(8,128)(2,1)S(1)} fusion(f32[2,512,1024]{2,1,0:T(8,128)} %get-tuple-element.12, f32[2,512]{1,0:T(2,128)S(1)} %get-tuple-element.11, bf16[1024,2,264]{0,2,1:T(8,128)(2,1)S(1)} %bitcast.53), kind=kOutput, calls=%fused_computation.48 | convolution fusion | flops 186736640 | bytes 4739072 | tf_op jit(solution)/shard_map/hqk,khd->qhd/dot_general | solution.py:43
  68.2 0.3 copy-done.13
  68.4 0.9 fusion.38
  69.3 0.2 copy-done.4
  69.5 2.7 %bitcast_convert_fusion = bf16[1024,1408]{1,0:T(8,128)(2,1)} fusion(bf16[2,88,1408]{2,1,0:T(8,128)(2,1)S(1)} %copy-done.4, bf16[512,2,88]{0,2,1:T(8,128)(2,1)S(1)} %fusion.38, bf16[512,2,88]{0,2,1:T(8,128)(2,1)S(1)} %fusion.37), kind=kOutput, calls=%fused_computation.20 | convolution fusion | flops 509673472 | bytes 3739648 | tf_op jit(solution)/shard_map/dot_general | solution.py:77
  72.1 0.0 all-reduce.2.cloned.1.call-update
  72.2 0.0 all-gather.7.cloned.1.call-start
  72.2 0.0 copy-done.5
  72.2 10.5 %all-gather = bf16[352,448]{1,0:T(8,128)(2,1)} all-gather(bf16[88,448]{1,0:T(8,128)(2,1)S(1)} %copy-done.5), channel_id=2, replica_groups=mesh['y'=4,'z'=16,'x'=4,'core'=2] {'y'}, dimensions={0}, use_global_device_ids=true | all-gather | bytes 394240 | tf_op jit(solution)/shard_map/all_gather | solution.py:63
  82.7 0.0 all-gather.7.cloned.1.call-update
  82.8 0.6 reduce-window.6
  83.4 0.2 slice_reduce_fusion
  83.6 0.1 fusion.74
  83.8 74.2 %all-reduce.2.cloned.1.call-done = bf16[1024,1408]{1,0:T(8,128)(2,1)} async-done(((bf16[1024,1408]{1,0:T(8,128)(2,1)}), bf16[1024,1408]{1,0:T(8,128)(2,1)}) %all-reduce.2.cloned.1.call-update) | async-done | bytes 2883600 | tf_op jit(solution)/shard_map/psum | solution.py:76
  158.0 3.7 %convert_reduce_fusion.1 = f32[1024]{0:T(1024)S(1)} fusion(bf16[1024,1408]{1,0:T(8,128)(2,1)} %all-reduce.2.cloned.1.call-done, bf16[1024,1408]{1,0:T(8,128)(2,1)} %all-gather.5.cloned.1.call-done), kind=kLoop, calls=%fused_computation.6 | loop fusion | flops 8649728 | bytes 5771264 | tf_op jit(solution)/shard_map/reduce_sum | solution.py:12
  161.7 0.0 copy-start.7
  161.7 0.0 copy-start.8
  161.7 0.7 copy-done.3
  162.5 1.2 fusion.10
  163.7 2.9 %fusion.13 = bf16[1024,1408]{1,0:T(8,128)(2,1)} fusion(f32[1408]{0:T(1024)S(1)} %copy-done.7, f32[1408]{0:T(1024)S(1)} %copy-done.8, f32[1024]{0:T(1024)S(1)} %add_rsqrt_fusion, f32[1024]{0:T(1024)S(1)} %broadcast_multiply_fusion, bf16[1024,1408]{1,0:T(8,128)(2,1)S(1)} %copy-done.3, bf16[1024,1408]{1,0:T(8,128)(2,1)S(1)} %copy-done.2), kind=kLoop, calls=%fused_computation.18 | loop fusion | flops 14417920 | bytes 8670208 | tf_op jit(solution)/shard_map/convert_element_type | solution.py:81
  166.6 5.6 %reshape.152 = bf16[256,5632]{1,0:T(8,128)(2,1)} reshape(bf16[1024,1408]{1,0:T(8,128)(2,1)} %fusion.13) | data formatting | bytes 5767168 | tf_op jit(solution)/shard_map/reshape | solution.py:83
  172.2 5.5 %convolution_convert_fusion = bf16[512,448]{0,1:T(8,128)(2,1)S(1)} fusion(bf16[256,5632]{1,0:T(8,128)(2,1)} %reshape.152, bf16[5632,448]{1,0:T(8,128)(2,1)} %bitcast.50, f32[448]{0:T(512)S(1)} %copy-done.11, s32[256]{0:T(256)S(1)} %multiply_add_fusion), kind=kOutput, calls=%fused_computation.43 | convolution fusion | flops 1409875968 | bytes 8391424 | tf_op jit(solution)/shard_map/dot_general | solution.py:97
  177.7 0.2 copy.13
  177.9 46.7 %all_to_all.5 = bf16[64,8,448]{2,1,0:T(8,128)(2,1)S(1)} all-to-all(bf16[64,8,448]{2,1,0:T(8,128)(2,1)S(1)} %bitcast.43), channel_id=1, replica_groups=mesh['y'=4,'z'=16,'x'=4,'core'=2] {'y','z'}, dimensions={0} | all-to-all | bytes 917504 | tf_op jit(solution)/shard_map/all_to_all | solution.py:101
  224.6 1.0 copy.14
  (25 shorter events, 0.1 us)
Async XLA Ops:
  7.4 44.8 %copy-start = (bf16[1408,2,264]{0,2,1:T(8,128)(2,1)S(1)}, bf16[1408,2,264]{0,2,1:T(8,128)(2,1)}, u32[]{:S(2)}) copy-start(bf16[1408,2,264]{0,2,1:T(8,128)(2,1)} %param.14) | copy-start | bytes 4460548
  7.4 44.8 %copy-start.10 = (f32[1408]{0:T(1024)S(1)}, f32[1408]{0:T(1024)}, u32[]{:S(2)}) copy-start(f32[1408]{0:T(1024)} %param.12) | copy-start | bytes 16900
  7.4 44.8 %copy-start.9 = (f32[1408]{0:T(1024)S(1)}, f32[1408]{0:T(1024)}, u32[]{:S(2)}) copy-start(f32[1408]{0:T(1024)} %param.13) | copy-start | bytes 16900
  7.4 41.2 %all-gather.5.cloned.1.call-start = ((), (), s32[]{:S(2)}) async-start(), calls=%async_computation.1 | async-start | bytes 3244032 | tf_op jit(solution)/shard_map/all_gather | solution.py:65
  8.1 149.9 %all-reduce.2.cloned.1.call-start = ((), (), s32[]{:S(2)}) async-start(), calls=%async_computation.2 | async-start | bytes 5767168 | tf_op jit(solution)/shard_map/psum | solution.py:76
  48.6 2.7 %copy-start.1 = (bf16[1024,1408]{1,0:T(8,128)(2,1)S(1)}, bf16[1024,1408]{1,0:T(8,128)(2,1)}, u32[]{:S(2)}) copy-start(bf16[1024,1408]{1,0:T(8,128)(2,1)} %all-gather.5.cloned.1.call-done) | copy-start | bytes 8650756
  60.1 4.9 %copy-start.12 = (bf16[1024,528]{0,1:T(8,128)(2,1)S(1)}, bf16[1024,528]{0,1:T(8,128)(2,1)}, u32[]{:S(2)}) copy-start(bf16[1024,528]{0,1:T(8,128)(2,1)} %fusion.31) | copy-start | bytes 3244036
  65.0 3.4 %copy-start.13 = (f32[2,512,1024]{2,1,0:T(8,128)S(1)}, f32[2,512,1024]{2,1,0:T(8,128)}, u32[]{:S(2)}) copy-start(f32[2,512,1024]{2,1,0:T(8,128)} %get-tuple-element.10) | copy-start | bytes 12582916
  68.4 1.0 copy-start.4
  69.5 2.8 %copy-start.5 = (bf16[88,448]{1,0:T(8,128)(2,1)S(1)}, bf16[88,448]{1,0:T(8,128)(2,1)}, u32[]{:S(2)}) copy-start(bf16[88,448]{1,0:T(8,128)(2,1)} %param.18) | copy-start | bytes 236548
  69.5 13.3 %copy-start.6 = (s32[256,1]{0,1:T(1,128)S(1)}, s32[256,1]{0,1:T(1,128)}, u32[]{:S(2)}) copy-start(s32[256,1]{0,1:T(1,128)} %param.21) | copy-start | bytes 3076
  72.2 100.1 %all-gather.7.cloned.1.call-start = ((), (), s32[]{:S(2)}) async-start(), calls=%async_computation.3 | async-start | bytes 6127616 | tf_op jit(solution)/shard_map/all_gather | solution.py:64
  158.0 3.7 %copy-start.2 = (bf16[1024,1408]{1,0:T(8,128)(2,1)S(1)}, bf16[1024,1408]{1,0:T(8,128)(2,1)}, u32[]{:S(2)}) copy-start(bf16[1024,1408]{1,0:T(8,128)(2,1)} %all-gather.5.cloned.1.call-done) | copy-start | bytes 8650756
  158.0 4.5 %copy-start.3 = (bf16[1024,1408]{1,0:T(8,128)(2,1)S(1)}, bf16[1024,1408]{1,0:T(8,128)(2,1)}, u32[]{:S(2)}) copy-start(bf16[1024,1408]{1,0:T(8,128)(2,1)} %all-reduce.2.cloned.1.call-done) | copy-start | bytes 8650756
  161.7 2.0 copy-start.7
  161.7 2.0 copy-start.8
  166.6 5.6 %copy-start.11 = (f32[448]{0:T(512)S(1)}, f32[448]{0:T(512)}, u32[]{:S(2)}) copy-start(f32[448]{0:T(512)} %param.19) | copy-start | bytes 5380
Sparse Core Ops, SparseCore 0:
  10.3 38.2 all-gather.4
  72.3 85.6 all-reduce.1
Sparse Core Ops, SparseCore 1:
  82.9 82.2 all-gather.6

commit v4 on v3

--- a/solution.py
+++ b/solution.py
@@ -73,14 +73,17 @@
     token_segs = jnp.repeat(segments[0], 4)
     context = attend(heads_qkv, token_segs).reshape(row_count, -1)
     out_flat = w_out.reshape(-1, w_out.shape[2])
-    attn_all = lax.psum(
-        jnp.dot(context, out_flat, preferred_element_type=jnp.float32).astype(jnp.bfloat16),
-        TP,
-    ).astype(jnp.float32)
-    hidden = (gathered.astype(jnp.float32) + attn_all).astype(jnp.bfloat16)
-    normed_all = layer_norm(hidden, ln2_gain, ln2_shift).astype(jnp.bfloat16)
-    groups = row_count // 4
-    merged = normed_all.reshape(groups, -1)
+    term = jnp.dot(context, out_flat, preferred_element_type=jnp.float32).astype(jnp.bfloat16)
+    tp_count = lax.axis_size("x") * lax.axis_size("core")
+    local_rows = tokens.shape[0]
+    terms_mine = lax.all_to_all(term.reshape(tp_count, local_rows, -1), TP, 0, 0, tiled=True)
+    attn = jnp.sum(terms_mine.astype(jnp.float32), axis=0)
+    hidden = (tokens.astype(jnp.float32) + attn).astype(jnp.bfloat16)
+    normed_two = layer_norm(hidden, ln2_gain, ln2_shift).astype(jnp.bfloat16)
+    merged_mine = normed_two.reshape(local_rows // 4, -1)
+    copies = jnp.broadcast_to(merged_mine[None], (tp_count,) + merged_mine.shape)
+    merged = lax.all_to_all(copies, TP, 0, 0, tiled=True).reshape(-1, merged_mine.shape[1])
+    groups = merged.shape[0]
     summed = jnp.dot(
         merged, w_proj_all, preferred_element_type=jnp.float32
     )

time: 233 us -> 214 us (0.918)
  the two profiles are of different devices: /device:TPU:15 before, /device:TPU:8 now
where the time goes in v4:
time: 214 us; the launch traced here: 213 us
  blocking collectives  104 us (49%)
  waiting for transfers between devices  55.7 us (26%)
  matrix products  23.3 us (11%)
  between operations  13.6 us (6%)
  local copies, waits for them, and re-layouts  6.29 us (3%)
  other arithmetic  5.86 us (3%)
  starting transfers between devices  4.65 us (2%)
    all_to_all x1, blocking collectives, shards(): lax.all_to_all(outgoing, DP, split_axis=0, concat_axis=0, tiled=True)  46.8 us
    all_to_all x1, blocking collectives, shards(): lax.all_to_all(term.reshape(tp_count, local_rows, -1), TP, 0, 0, tiled=True)  39.4 us
    all_gather x1, waiting for transfers between devices, shards(): gathered = lax.all_gather(tokens, TP, axis=0, tiled=True)  20.6 us
    all_to_all x1, waiting for transfers between devices, shards(): lax.all_to_all(copies, TP, 0, 0, tiled=True)  18.2 us
    all_gather x1, blocking collectives, shards(): w_y = lax.all_gather(w_proj, 'y', axis=0)  17.7 us
    all_gather x1, waiting for transfers between devices, shards(): w_proj_all = lax.all_gather(w_y, 'z', axis=1).reshape(-1, w_proj.shape[1])  16.2 us
    sub x2, matrix products, attend(): exponent = jnp.exp(scores - row_max)  9.62 us
    dot_general x1, matrix products, shards(): jnp.dot(scatter_table, projected, preferred_element_type=jnp.float32)  5.46 us
  transfers between devices with their start and end apart: 3, of which 3 were waited for; matrix products, arithmetic and copies ran while one was open for 13% of the time, Pallas kernels for 0%

profile of v4, /device:TPU:8, one launch (start us, length us, event | category | flops | bytes accessed | tf_op | source)
XLA Modules:
  0.0 213.3 jit_solution(13098312652637670805)
XLA Ops:
  6.5 0.0 copy-start
  6.5 0.7 all-gather.5.cloned.1.call-update
  7.3 0.0 all-gather.7.cloned.1.call-start
  7.3 17.7 %all-gather = bf16[352,448]{1,0:T(8,128)(2,1)} all-gather(bf16[88,448]{1,0:T(8,128)(2,1)} %param.18), channel_id=2, replica_groups=mesh['y'=4,'z'=16,'x'=4,'core'=2] {'y'}, dimensions={0}, use_global_device_ids=true | all-gather | bytes 394240 | tf_op jit(solution)/shard_map/all_gather | solution.py:63
  25.0 0.0 all-gather.7.cloned.1.call-update
  25.0 0.7 slice_bitcast_fusion.1
  25.7 0.1 broadcast_in_dim.28
  25.8 0.1 eq.84
  25.9 0.1 broadcast_in_dim.56
  26.0 0.1 eq.89
  26.1 0.8 broadcast_in_dim.29
  26.9 0.1 eq.86
  27.0 0.7 broadcast_compare_fusion.1
  27.7 20.6 %all-gather.5.cloned.1.call-done = bf16[1024,1408]{1,0:T(8,128)(2,1)} async-done(((bf16[128,1408]{1,0:T(8,128)(2,1)}), bf16[1024,1408]{1,0:T(8,128)(2,1)}) %all-gather.5.cloned.1.call-update) | async-done | bytes 2883600 | tf_op jit(solution)/shard_map/all_gather | solution.py:65
  48.2 2.4 %convert_reduce_fusion = f32[1024]{0:T(1024)S(1)} fusion(bf16[1024,1408]{1,0:T(8,128)(2,1)} %all-gather.5.cloned.1.call-done), kind=kLoop, calls=%fused_computation.3 | loop fusion | flops 2882560 | bytes 2887680 | tf_op jit(solution)/shard_map/reduce_sum | solution.py:12
  50.6 0.3 copy-done.1
  50.9 0.9 fusion.4
  51.8 3.1 %fusion.24 = bf16[1024,528]{0,1:T(8,128)(2,1)} fusion(bf16[1408,528]{0,1:T(8,128)(2,1)S(1)} %bitcast.44, bf16[1024,1408]{1,0:T(8,128)(2,1)S(1)} %copy-done.1, f32[1408]{0:T(1024)S(1)} %copy-done.7, f32[1408]{0:T(1024)S(1)} %copy-done.8, f32[1024]{0:T(1024)S(1)} %add_rsqrt_fusion, f32[1024]{0:T(1024)S(1)} %broadcast_multiply_fusion), kind=kOutput, calls=%fused_computation.33 | convolution fusion | flops 1531723776 | bytes 5471232 | tf_op jit(solution)/shard_map/dot_general | solution.py:69
  55.0 4.8 %fusion.89 = (f32[2,512]{1,0:T(2,128)S(1)}, f32[2,512,1024]{2,1,0:T(8,128)}) fusion(pred[512,1024]{1,0:T(8,128)(4,1)S(1)} %get-tuple-element.7, bf16[1024,2,264]{0,2,1:T(8,128)(2,1)} %bitcast.54), kind=kOutput, calls=%fused_computation.94 | convolution fusion | flops 188744704 | bytes 5263360 | tf_op jit(solution)/shard_map/sub | solution.py:41
  59.8 4.8 %fusion.80 = (f32[2,512]{1,0:T(2,128)S(1)}, f32[2,512,1024]{2,1,0:T(8,128)}) fusion(pred[512,1024]{1,0:T(8,128)(4,1)S(1)} %get-tuple-element.8, bf16[1024,2,264]{0,2,1:T(8,128)(2,1)} %bitcast.55), kind=kOutput, calls=%fused_computation.93 | convolution fusion | flops 188744704 | bytes 5263360 | tf_op jit(solution)/shard_map/sub | solution.py:41
  64.6 3.2 %fusion.30 = bf16[512,2,88]{0,2,1:T(8,128)(2,1)S(1)} fusion(f32[2,512,1024]{2,1,0:T(8,128)} %get-tuple-element.14, f32[2,512]{1,0:T(2,128)S(1)} %get-tuple-element.13, bf16[1024,2,264]{0,2,1:T(8,128)(2,1)S(1)} %bitcast.56), kind=kOutput, calls=%fused_computation.39 | convolution fusion | flops 186736640 | bytes 4739072 | tf_op jit(solution)/shard_map/hqk,khd->qhd/dot_general | solution.py:43
  67.8 0.4 copy-done.11
  68.2 0.9 fusion.31
  69.0 0.2 copy-done.3
  69.2 1.0 bitcast_convert_fusion
  70.2 0.0 copy-start.2
  70.2 0.0 copy-start.5
  70.2 0.0 copy-start.6
  70.2 39.4 %all_to_all.15 = bf16[8,128,1408]{2,1,0:T(8,128)(2,1)S(1)} all-to-all(bf16[8,128,1408]{2,1,0:T(8,128)(2,1)S(1)} %bitcast.45), channel_id=1, replica_groups=mesh['y'=4,'z'=16,'x'=4,'core'=2] {'x','core'}, dimensions={0} | all-to-all | bytes 5767168 | tf_op jit(solution)/shard_map/all_to_all | solution.py:79
  109.6 0.4 convert_reduce_fusion.1
  110.0 0.0 copy-done.2
  110.0 0.2 convert_reduce_fusion.2
  110.2 0.2 fusion.34
  110.5 0.3 fusion.37
  110.8 0.2 broadcast_in_dim.58
  111.0 0.0 copy-start.4
  111.1 0.0 copy-start.9
  111.1 1.9 broadcast_in_dim.59
  113.0 4.6 %all-to-all-start.1 = ((bf16[8,32,5632]{2,1,0:T(8,128)(2,1)}), bf16[8,32,5632]{2,1,0:T(8,128)(2,1)}, u32[]{:S(2)}, u32[]{:S(2)}) async-start(bf16[8,32,5632]{2,1,0:T(8,128)(2,1)} %broadcast_in_dim.59), calls=%async_computation.1 | async-start | bytes 5767168 | tf_op jit(solution)/shard_map/all_to_all | solution.py:85
  117.6 0.6 reduce-window.6
  118.2 0.2 slice_reduce_fusion
  118.4 0.1 fusion.73
  118.6 16.2 %all-gather.7.cloned.1.call-done = bf16[4,1408,448]{2,1,0:T(8,128)(2,1)} async-done(((bf16[4,88,448]{2,1,0:T(8,128)(2,1)}), bf16[4,1408,448]{2,1,0:T(8,128)(2,1)}) %all-gather.7.cloned.1.call-update) | async-done | bytes 5046288 | tf_op jit(solution)/shard_map/all_gather | solution.py:64
  134.8 18.2 %all-to-all-done.1 = bf16[8,32,5632]{2,1,0:T(8,128)(2,1)} async-done(((bf16[8,32,5632]{2,1,0:T(8,128)(2,1)}), bf16[8,32,5632]{2,1,0:T(8,128)(2,1)}, u32[]{:S(2)}, u32[]{:S(2)}) %all-to-all-start.1) | async-done | bytes 2883616 | tf_op jit(solution)/shard_map/all_to_all | solution.py:85
  153.0 5.5 %convolution_convert_fusion = bf16[512,448]{0,1:T(8,128)(2,1)S(1)} fusion(bf16[256,5632]{1,0:T(8,128)(2,1)} %bitcast.12, bf16[5632,448]{1,0:T(8,128)(2,1)} %bitcast.53, f32[448]{0:T(512)S(1)} %copy-done.9, s32[256]{0:T(256)S(1)} %multiply_add_fusion), kind=kOutput, calls=%fused_computation.34 | convolution fusion | flops 1409875968 | bytes 8391424 | tf_op jit(solution)/shard_map/dot_general | solution.py:100
  158.5 0.2 copy.13
  158.7 46.8 %all_to_all.16 = bf16[64,8,448]{2,1,0:T(8,128)(2,1)S(1)} all-to-all(bf16[64,8,448]{2,1,0:T(8,128)(2,1)S(1)} %bitcast.46), channel_id=1, replica_groups=mesh['y'=4,'z'=16,'x'=4,'core'=2] {'y','z'}, dimensions={0} | all-to-all | bytes 917504 | tf_op jit(solution)/shard_map/all_to_all | solution.py:104
  205.5 1.0 copy.14
  (23 shorter events, 0.1 us)
Async XLA Ops:
  6.5 45.3 %copy-start = (bf16[1408,2,264]{0,2,1:T(8,128)(2,1)S(1)}, bf16[1408,2,264]{0,2,1:T(8,128)(2,1)}, u32[]{:S(2)}) copy-start(bf16[1408,2,264]{0,2,1:T(8,128)(2,1)} %param.14) | copy-start | bytes 4460548
  6.5 41.7 %all-gather.5.cloned.1.call-start = ((), (), s32[]{:S(2)}) async-start(), calls=%async_computation.3 | async-start | bytes 3244032 | tf_op jit(solution)/shard_map/all_gather | solution.py:65
  7.3 44.6 %copy-start.7 = (f32[1408]{0:T(1024)S(1)}, f32[1408]{0:T(1024)}, u32[]{:S(2)}) copy-start(f32[1408]{0:T(1024)} %param.13) | copy-start | bytes 16900
  7.3 44.6 %copy-start.8 = (f32[1408]{0:T(1024)S(1)}, f32[1408]{0:T(1024)}, u32[]{:S(2)}) copy-start(f32[1408]{0:T(1024)} %param.12) | copy-start | bytes 16900
  7.3 127.5 %all-gather.7.cloned.1.call-start = ((), (), s32[]{:S(2)}) async-start(), calls=%async_computation.4 | async-start | bytes 6127616 | tf_op jit(solution)/shard_map/all_gather | solution.py:64
  48.2 2.7 %copy-start.1 = (bf16[1024,1408]{1,0:T(8,128)(2,1)S(1)}, bf16[1024,1408]{1,0:T(8,128)(2,1)}, u32[]{:S(2)}) copy-start(bf16[1024,1408]{1,0:T(8,128)(2,1)} %all-gather.5.cloned.1.call-done) | copy-start | bytes 8650756
  59.8 4.8 %copy-start.10 = (bf16[1024,528]{0,1:T(8,128)(2,1)S(1)}, bf16[1024,528]{0,1:T(8,128)(2,1)}, u32[]{:S(2)}) copy-start(bf16[1024,528]{0,1:T(8,128)(2,1)} %fusion.24) | copy-start | bytes 3244036
  64.6 3.6 %copy-start.11 = (f32[2,512,1024]{2,1,0:T(8,128)S(1)}, f32[2,512,1024]{2,1,0:T(8,128)}, u32[]{:S(2)}) copy-start(f32[2,512,1024]{2,1,0:T(8,128)} %get-tuple-element.12) | copy-start | bytes 12582916
  68.2 1.0 copy-start.3
  70.2 39.8 %copy-start.2 = (bf16[128,1408]{1,0:T(8,128)(2,1)S(1)}, bf16[128,1408]{1,0:T(8,128)(2,1)}, u32[]{:S(2)}) copy-start(bf16[128,1408]{1,0:T(8,128)(2,1)} %param.11) | copy-start | bytes 1081348
  70.2 40.3 %copy-start.5 = (f32[1408]{0:T(1024)S(1)}, f32[1408]{0:T(1024)}, u32[]{:S(2)}) copy-start(f32[1408]{0:T(1024)} %param.17) | copy-start | bytes 16900
  70.2 40.3 %copy-start.6 = (f32[1408]{0:T(1024)S(1)}, f32[1408]{0:T(1024)}, u32[]{:S(2)}) copy-start(f32[1408]{0:T(1024)} %param.16) | copy-start | bytes 16900
  111.0 6.5 %copy-start.4 = (s32[256,1]{0,1:T(1,128)S(1)}, s32[256,1]{0,1:T(1,128)}, u32[]{:S(2)}) copy-start(s32[256,1]{0,1:T(1,128)} %param.21) | copy-start | bytes 3076
  111.1 42.0 %copy-start.9 = (f32[448]{0:T(512)S(1)}, f32[448]{0:T(512)}, u32[]{:S(2)}) copy-start(f32[448]{0:T(512)} %param.19) | copy-start | bytes 5380
  113.0 40.1 %all-to-all-start.1 = ((bf16[8,32,5632]{2,1,0:T(8,128)(2,1)}), bf16[8,32,5632]{2,1,0:T(8,128)(2,1)}, u32[]{:S(2)}, u32[]{:S(2)}) async-start(bf16[8,32,5632]{2,1,0:T(8,128)(2,1)} %broadcast_in_dim.59), calls=%async_computation.1 | async-start | bytes 5767168 | tf_op jit(solution)/shard_map/all_to_all | solution.py:85
Sparse Core Ops, SparseCore 0:
  9.5 38.6 all-gather.4
  50.3 84.4 all-gather.6

commit v5 on v4

--- a/solution.py
+++ b/solution.py
@@ -62,9 +62,9 @@
     ny, nz = lax.axis_size("y"), lax.axis_size("z")
     w_y = lax.all_gather(w_proj, "y", axis=0)
     w_proj_all = lax.all_gather(w_y, "z", axis=1).reshape(-1, w_proj.shape[1])
-    gathered = lax.all_gather(tokens, TP, axis=0, tiled=True)
-    row_count = gathered.shape[0]
-    normed = layer_norm(gathered, ln1_gain, ln1_shift).astype(jnp.bfloat16)
+    normed_mine = layer_norm(tokens, ln1_gain, ln1_shift).astype(jnp.bfloat16)
+    normed = lax.all_gather(normed_mine, TP, axis=0, tiled=True)
+    row_count = normed.shape[0]
     heads_here = w_qkv.shape[1]
     heads_qkv = jnp.dot(
         normed, w_qkv.reshape(w_qkv.shape[0], -1), preferred_element_type=jnp.float32

time: 214 us -> 214 us (level)
  transfers between devices with their start and end apart: 3 -> 3, of which waited for: 3 -> 3; matrix products, arithmetic and copies ran while one was open for 13% -> 12% of each run, Pallas kernels for 0% -> 0%
where the time goes in v5:
time: 214 us; the launch traced here: 213 us
  blocking collectives  104 us (49%)
  waiting for transfers between devices  53.8 us (25%)
  matrix products  24.8 us (12%)
  between operations  13.5 us (6%)
  other arithmetic  7.05 us (3%)
  local copies, waits for them, and re-layouts  5.79 us (3%)
  starting transfers between devices  4.6 us (2%)
    all_to_all x1, blocking collectives, shards(): lax.all_to_all(outgoing, DP, split_axis=0, concat_axis=0, tiled=True)  46.8 us
    all_to_all x1, blocking collectives, shards(): lax.all_to_all(term.reshape(tp_count, local_rows, -1), TP, 0, 0, tiled=True)  39.4 us
    all_gather x1, waiting for transfers between devices, shards(): normed = lax.all_gather(normed_mine, TP, axis=0, tiled=True)  19.1 us
    all_gather x1, waiting for transfers between devices, shards(): w_proj_all = lax.all_gather(w_y, 'z', axis=1).reshape(-1, w_proj.shape[1])  17.8 us
    all_gather x1, blocking collectives, shards(): w_y = lax.all_gather(w_proj, 'y', axis=0)  17.7 us
    all_to_all x1, waiting for transfers between devices, shards(): lax.all_to_all(copies, TP, 0, 0, tiled=True)  16.8 us
    sub x2, matrix products, attend(): exponent = jnp.exp(scores - row_max)  9.61 us
    dot_general x1, matrix products, shards(): jnp.dot(scatter_table, projected, preferred_element_type=jnp.float32)  5.45 us
  transfers between devices with their start and end apart: 3, of which 3 were waited for; matrix products, arithmetic and copies ran while one was open for 12% of the time, Pallas kernels for 0%

profile of v5, /device:TPU:8, one launch (start us, length us, event | category | flops | bytes accessed | tf_op | source)
XLA Modules:
  0.0 213.5 jit_solution(7174860456725009823)
XLA Ops:
  6.5 0.0 copy-start
  6.5 0.0 all-gather.5.cloned.1.call-start
  6.5 1.2 convert_reduce_fusion.1
  7.8 1.2 fusion.21
  9.0 2.0 fusion.24
  11.1 0.0 all-gather.5.cloned.1.call-update
  11.1 0.0 all-gather.7.cloned.1.call-start
  11.1 17.7 %all-gather = bf16[352,448]{1,0:T(8,128)(2,1)} all-gather(bf16[88,448]{1,0:T(8,128)(2,1)} %param.18), channel_id=2, replica_groups=mesh['y'=4,'z'=16,'x'=4,'core'=2] {'y'}, dimensions={0}, use_global_device_ids=true | all-gather | bytes 394240 | tf_op jit(solution)/shard_map/all_gather | solution.py:63
  28.8 0.0 all-gather.7.cloned.1.call-update
  28.8 0.7 slice_bitcast_fusion.1
  29.5 0.1 broadcast_in_dim.28
  29.6 0.1 eq.84
  29.7 0.1 broadcast_in_dim.56
  29.8 0.1 eq.89
  29.9 0.0 copy-done.6
  29.9 0.1 broadcast_in_dim.29
  30.0 0.1 eq.86
  30.1 0.7 broadcast_compare_fusion.1
  30.8 19.1 %all-gather.5.cloned.1.call-done = bf16[1024,1408]{1,0:T(8,128)(2,1)} async-done(((bf16[128,1408]{1,0:T(8,128)(2,1)}), bf16[1024,1408]{1,0:T(8,128)(2,1)}) %all-gather.5.cloned.1.call-update) | async-done | bytes 2883600 | tf_op jit(solution)/shard_map/all_gather | solution.py:66
  49.9 0.0 copy-done
  49.9 4.7 %convolution_convert_fusion = bf16[1024,528]{0,1:T(8,128)(2,1)} fusion(bf16[1024,1408]{1,0:T(8,128)(2,1)} %all-gather.5.cloned.1.call-done, bf16[1408,528]{0,1:T(8,128)(2,1)S(1)} %bitcast.45), kind=kOutput, calls=%fused_computation.20 | convolution fusion | flops 1523073024 | bytes 5451776 | tf_op jit(solution)/shard_map/dot_general | solution.py:69
  54.6 4.8 %fusion.82 = (f32[2,512]{1,0:T(2,128)S(1)}, f32[2,512,1024]{2,1,0:T(8,128)}) fusion(pred[512,1024]{1,0:T(8,128)(4,1)S(1)} %get-tuple-element.7, bf16[1024,2,264]{0,2,1:T(8,128)(2,1)} %bitcast.55), kind=kOutput, calls=%fused_computation.90 | convolution fusion | flops 188744704 | bytes 5263360 | tf_op jit(solution)/shard_map/sub | solution.py:41
  59.4 4.8 %fusion.73 = (f32[2,512]{1,0:T(2,128)S(1)}, f32[2,512,1024]{2,1,0:T(8,128)}) fusion(pred[512,1024]{1,0:T(8,128)(4,1)S(1)} %get-tuple-element.8, bf16[1024,2,264]{0,2,1:T(8,128)(2,1)} %bitcast.56), kind=kOutput, calls=%fused_computation.89 | convolution fusion | flops 188744704 | bytes 5263360 | tf_op jit(solution)/shard_map/sub | solution.py:41
  64.2 0.0 copy-done.8
  64.2 3.2 %fusion.15 = bf16[512,2,88]{0,2,1:T(8,128)(2,1)S(1)} fusion(f32[2,512,1024]{2,1,0:T(8,128)} %get-tuple-element.14, f32[2,512]{1,0:T(2,128)S(1)} %get-tuple-element.13, bf16[1024,2,264]{0,2,1:T(8,128)(2,1)S(1)} %bitcast.57), kind=kOutput, calls=%fused_computation.26 | convolution fusion | flops 186736640 | bytes 4739072 | tf_op jit(solution)/shard_map/hqk,khd->qhd/dot_general | solution.py:43
  67.4 0.3 copy-done.9
  67.7 0.9 fusion.16
  68.6 0.2 copy-done.2
  68.7 1.0 bitcast_convert_fusion
  69.7 39.4 %all_to_all.15 = bf16[8,128,1408]{2,1,0:T(8,128)(2,1)S(1)} all-to-all(bf16[8,128,1408]{2,1,0:T(8,128)(2,1)S(1)} %bitcast.46), channel_id=1, replica_groups=mesh['y'=4,'z'=16,'x'=4,'core'=2] {'x','core'}, dimensions={0} | all-to-all | bytes 5767168 | tf_op jit(solution)/shard_map/all_to_all | solution.py:79
  109.1 0.4 convert_reduce_fusion
  109.5 0.6 copy-done.1
  110.1 0.2 convert_reduce_fusion.2
  110.3 0.2 fusion.25
  110.6 0.3 fusion.28
  110.9 0.2 broadcast_in_dim.58
  111.1 1.9 broadcast_in_dim.59
  113.0 4.6 %all-to-all-start.1 = ((bf16[8,32,5632]{2,1,0:T(8,128)(2,1)}), bf16[8,32,5632]{2,1,0:T(8,128)(2,1)}, u32[]{:S(2)}, u32[]{:S(2)}) async-start(bf16[8,32,5632]{2,1,0:T(8,128)(2,1)} %broadcast_in_dim.59), calls=%async_computation.1 | async-start | bytes 5767168 | tf_op jit(solution)/shard_map/all_to_all | solution.py:85
  117.6 0.0 copy-done.3
  117.6 0.6 reduce-window.6
  118.2 0.2 slice_reduce_fusion
  118.4 0.1 fusion.65
  118.6 17.8 %all-gather.7.cloned.1.call-done = bf16[4,1408,448]{2,1,0:T(8,128)(2,1)} async-done(((bf16[4,88,448]{2,1,0:T(8,128)(2,1)}), bf16[4,1408,448]{2,1,0:T(8,128)(2,1)}) %all-gather.7.cloned.1.call-update) | async-done | bytes 5046288 | tf_op jit(solution)/shard_map/all_gather | solution.py:64
  136.4 16.8 %all-to-all-done.1 = bf16[8,32,5632]{2,1,0:T(8,128)(2,1)} async-done(((bf16[8,32,5632]{2,1,0:T(8,128)(2,1)}), bf16[8,32,5632]{2,1,0:T(8,128)(2,1)}, u32[]{:S(2)}, u32[]{:S(2)}) %all-to-all-start.1) | async-done | bytes 2883616 | tf_op jit(solution)/shard_map/all_to_all | solution.py:85
  153.2 5.5 %convolution_convert_fusion.1 = bf16[512,448]{0,1:T(8,128)(2,1)S(1)} fusion(bf16[256,5632]{1,0:T(8,128)(2,1)} %bitcast.12, bf16[5632,448]{1,0:T(8,128)(2,1)} %bitcast.54, f32[448]{0:T(512)S(1)} %copy-done.7, s32[256]{0:T(256)S(1)} %multiply_add_fusion), kind=kOutput, calls=%fused_computation.21 | convolution fusion | flops 1409875968 | bytes 8391424 | tf_op jit(solution)/shard_map/dot_general | solution.py:100
  158.7 0.2 copy.13
  158.9 46.8 %all_to_all.16 = bf16[64,8,448]{2,1,0:T(8,128)(2,1)S(1)} all-to-all(bf16[64,8,448]{2,1,0:T(8,128)(2,1)S(1)} %bitcast.47), channel_id=1, replica_groups=mesh['y'=4,'z'=16,'x'=4,'core'=2] {'y','z'}, dimensions={0} | all-to-all | bytes 917504 | tf_op jit(solution)/shard_map/all_to_all | solution.py:104
  205.7 1.0 copy.14
  (20 shorter events, 0.1 us)
Async XLA Ops:
  6.5 43.4 %copy-start = (bf16[1408,2,264]{0,2,1:T(8,128)(2,1)S(1)}, bf16[1408,2,264]{0,2,1:T(8,128)(2,1)}, u32[]{:S(2)}) copy-start(bf16[1408,2,264]{0,2,1:T(8,128)(2,1)} %param.14) | copy-start | bytes 4460548
  6.5 23.4 %copy-start.6 = (s32[1,256]{1,0:T(1,128)S(1)}, s32[1,256]{1,0:T(1,128)}, u32[]{:S(2)}) copy-start(s32[1,256]{1,0:T(1,128)} %param.20) | copy-start | bytes 3076
  6.5 43.4 %all-gather.5.cloned.1.call-start = ((), (), s32[]{:S(2)}) async-start(), calls=%async_computation.3 | async-start | bytes 3244032 | tf_op jit(solution)/shard_map/all_gather | solution.py:66
  11.1 125.3 %all-gather.7.cloned.1.call-start = ((), (), s32[]{:S(2)}) async-start(), calls=%async_computation.4 | async-start | bytes 6127616 | tf_op jit(solution)/shard_map/all_gather | solution.py:64
  59.4 4.8 %copy-start.8 = (bf16[1024,528]{0,1:T(8,128)(2,1)S(1)}, bf16[1024,528]{0,1:T(8,128)(2,1)}, u32[]{:S(2)}) copy-start(bf16[1024,528]{0,1:T(8,128)(2,1)} %convolution_convert_fusion) | copy-start | bytes 3244036
  64.2 3.4 %copy-start.9 = (f32[2,512,1024]{2,1,0:T(8,128)S(1)}, f32[2,512,1024]{2,1,0:T(8,128)}, u32[]{:S(2)}) copy-start(f32[2,512,1024]{2,1,0:T(8,128)} %get-tuple-element.12) | copy-start | bytes 12582916
  67.7 1.0 copy-start.2
  109.1 1.0 copy-start.1
  109.1 1.4 copy-start.4
  109.1 1.4 copy-start.5
  113.0 4.6 %copy-start.3 = (s32[256,1]{0,1:T(1,128)S(1)}, s32[256,1]{0,1:T(1,128)}, u32[]{:S(2)}) copy-start(s32[256,1]{0,1:T(1,128)} %param.21) | copy-start | bytes 3076
  113.0 40.2 %copy-start.7 = (f32[448]{0:T(512)S(1)}, f32[448]{0:T(512)}, u32[]{:S(2)}) copy-start(f32[448]{0:T(512)} %param.19) | copy-start | bytes 5380
  113.0 40.2 %all-to-all-start.1 = ((bf16[8,32,5632]{2,1,0:T(8,128)(2,1)}), bf16[8,32,5632]{2,1,0:T(8,128)(2,1)}, u32[]{:S(2)}, u32[]{:S(2)}) async-start(bf16[8,32,5632]{2,1,0:T(8,128)(2,1)} %broadcast_in_dim.59), calls=%async_computation.1 | async-start | bytes 5767168 | tf_op jit(solution)/shard_map/all_to_all | solution.py:85
Sparse Core Ops, SparseCore 0:
  11.2 38.6 all-gather.4
  52.0 84.3 all-gather.6

commit v6 on v4

--- a/solution.py
+++ b/solution.py
@@ -63,6 +63,9 @@
     w_y = lax.all_gather(w_proj, "y", axis=0)
     w_proj_all = lax.all_gather(w_y, "z", axis=1).reshape(-1, w_proj.shape[1])
     gathered = lax.all_gather(tokens, TP, axis=0, tiled=True)
+    tp_n = lax.axis_size("x") * lax.axis_size("core")
+    w_out_all = lax.all_to_all(jnp.broadcast_to(w_out[None], (tp_n,) + w_out.shape), TP, 0, 0, tiled=True)
+    w_out_all = w_out_all.reshape((-1,) + w_out.shape[1:])
     row_count = gathered.shape[0]
     normed = layer_norm(gathered, ln1_gain, ln1_shift).astype(jnp.bfloat16)
     heads_here = w_qkv.shape[1]
@@ -72,12 +75,11 @@
     heads_qkv = heads_qkv.astype(jnp.bfloat16).reshape(row_count, heads_here, -1)
     token_segs = jnp.repeat(segments[0], 4)
     context = attend(heads_qkv, token_segs).reshape(row_count, -1)
-    out_flat = w_out.reshape(-1, w_out.shape[2])
-    term = jnp.dot(context, out_flat, preferred_element_type=jnp.float32).astype(jnp.bfloat16)
     tp_count = lax.axis_size("x") * lax.axis_size("core")
     local_rows = tokens.shape[0]
-    terms_mine = lax.all_to_all(term.reshape(tp_count, local_rows, -1), TP, 0, 0, tiled=True)
-    attn = jnp.sum(terms_mine.astype(jnp.float32), axis=0)
+    context_mine = lax.all_to_all(context.reshape(tp_count, local_rows, -1), TP, 0, 0, tiled=True)
+    out_heads = w_out_all.reshape(tp_count, -1, w_out_all.shape[2])
+    attn = jnp.einsum("sqd,sdo->qo", context_mine, out_heads, preferred_element_type=jnp.float32)
     hidden = (tokens.astype(jnp.float32) + attn).astype(jnp.bfloat16)
     normed_two = layer_norm(hidden, ln2_gain, ln2_shift).astype(jnp.bfloat16)
     merged_mine = normed_two.reshape(local_rows // 4, -1)

time: 214 us -> 207 us (0.967)
  blocking collectives: 104 us -> 71.5 us
  waiting for transfers between devices: 55.7 us -> 73.5 us
  starting transfers between devices: 4.65 us -> 9.32 us
    all_to_all x1, blocking collectives: 39.4 us -> 11 us  [shards(): lax.all_to_all(context.reshape(tp_count, local_rows, -1), TP, 0, 0, tiled...]
    all_to_all x1, waiting for transfers between devices: 18.2 us -> 34.5 us  [shards(): lax.all_to_all(copies, TP, 0, 0, tiled=True)]
    all_gather x1, waiting for transfers between devices: 16.2 us -> 3.99 us  [shards(): w_proj_all = lax.all_gather(w_y, 'z', axis=1).reshape(-1, w_proj.shape[1])]
    all_gather x1, waiting for transfers between devices: 20.6 us -> 28.7 us  [shards(): gathered = lax.all_gather(tokens, TP, axis=0, tiled=True)]
    all_to_all x0 -> x1, waiting for transfers between devices: none -> 5.62 us  [shards(): lax.all_to_all(jnp.broadcast_to(w_out[None], (tp_n,) + w_out.shape), TP,...]
    all_to_all x0 -> x1, starting transfers between devices: none -> 4.68 us  [shards(): lax.all_to_all(jnp.broadcast_to(w_out[None], (tp_n,) + w_out.shape), TP,...]
    all_to_all x1, blocking collectives: 46.8 us -> 42.8 us  [shards(): lax.all_to_all(outgoing, DP, split_axis=0, concat_axis=0, tiled=True)]
    broadcast_in_dim x0 -> x1, local copies, waits for them, and re-layouts: none -> 3.22 us  [shards(): jnp.broadcast_to(w_out[None], (tp_n,) + w_out.shape)]
  transfers between devices with their start and end apart: 3 -> 4, of which waited for: 3 -> 4; matrix products, arithmetic and copies ran while one was open for 13% -> 15% of each run, Pallas kernels for 0% -> 0%
where the time goes in v6:
time: 207 us; the launch traced here: 206 us
  waiting for transfers between devices  73.5 us (36%)
  blocking collectives  71.5 us (35%)
  matrix products  25.3 us (12%)
  between operations  13.7 us (7%)
  starting transfers between devices  9.32 us (5%)
  local copies, waits for them, and re-layouts  7.99 us (4%)
  other arithmetic  5.22 us (3%)
    all_to_all x1, blocking collectives, shards(): lax.all_to_all(outgoing, DP, split_axis=0, concat_axis=0, tiled=True)  42.8 us
    all_to_all x1, waiting for transfers between devices, shards(): lax.all_to_all(copies, TP, 0, 0, tiled=True)  34.5 us
    all_gather x1, waiting for transfers between devices, shards(): gathered = lax.all_gather(tokens, TP, axis=0, tiled=True)  28.7 us
    all_gather x1, blocking collectives, shards(): w_y = lax.all_gather(w_proj, 'y', axis=0)  17.7 us
    all_to_all x1, blocking collectives, shards(): lax.all_to_all(context.reshape(tp_count, local_rows, -1), TP, 0, 0, tiled...  11 us
    sub x2, matrix products, attend(): exponent = jnp.exp(scores - row_max)  9.62 us
    all_to_all x1, waiting for transfers between devices, shards(): lax.all_to_all(jnp.broadcast_to(w_out[None], (tp_n,) + w_out.shape), TP,...  5.62 us
    dot_general x1, matrix products, shards(): jnp.dot(scatter_table, projected, preferred_element_type=jnp.float32)  5.45 us
  transfers between devices with their start and end apart: 4, of which 4 were waited for; matrix products, arithmetic and copies ran while one was open for 15% of the time, Pallas kernels for 0%

profile of v6, /device:TPU:8, one launch (start us, length us, event | category | flops | bytes accessed | tf_op | source)
XLA Modules:
  0.0 206.5 jit_solution(6734756820148329865)
XLA Ops:
  6.5 0.0 copy-start
  6.5 0.7 all-gather.5.cloned.1.call-update
  7.3 0.0 all-gather.7.cloned.1.call-start
  7.3 17.7 %all-gather = bf16[352,448]{1,0:T(8,128)(2,1)} all-gather(bf16[88,448]{1,0:T(8,128)(2,1)} %param.18), channel_id=2, replica_groups=mesh['y'=4,'z'=16,'x'=4,'core'=2] {'y'}, dimensions={0}, use_global_device_ids=true | all-gather | bytes 394240 | tf_op jit(solution)/shard_map/all_gather | solution.py:63
  25.0 0.0 all-gather.7.cloned.1.call-update
  25.0 3.2 %broadcast_in_dim.64 = bf16[8,2,88,1408]{3,2,1,0:T(8,128)(2,1)} broadcast(bf16[2,88,1408]{2,1,0:T(8,128)(2,1)} %param.15), dimensions={1,2,3} | broadcast | bytes 4460544 | tf_op jit(solution)/shard_map/broadcast_in_dim | solution.py:67
  28.2 4.7 %all-to-all-start.1 = ((bf16[8,2,88,1408]{3,2,1,0:T(8,128)(2,1)}), bf16[8,2,88,1408]{3,2,1,0:T(8,128)(2,1)}, u32[]{:S(2)}, u32[]{:S(2)}) async-start(bf16[8,2,88,1408]{3,2,1,0:T(8,128)(2,1)} %broadcast_in_dim.64), calls=%async_computation.1 | async-start | bytes 7929856 | tf_op jit(solution)/shard_map/all_to_all | solution.py:67
  32.9 0.0 copy-start.7
  32.9 0.0 copy-start.8
  33.0 0.1 broadcast_in_dim.30
  33.0 0.1 eq.84
  33.2 0.1 broadcast_in_dim.34
  33.2 0.1 eq.89
  33.4 0.1 broadcast_in_dim.31
  33.4 0.1 eq.86
  33.6 0.7 broadcast_compare_fusion.1
  34.2 28.7 %all-gather.5.cloned.1.call-done = bf16[1024,1408]{1,0:T(8,128)(2,1)} async-done(((bf16[128,1408]{1,0:T(8,128)(2,1)}), bf16[1024,1408]{1,0:T(8,128)(2,1)}) %all-gather.5.cloned.1.call-update) | async-done | bytes 2883600 | tf_op jit(solution)/shard_map/all_gather | solution.py:65
  63.0 2.4 %convert_reduce_fusion = f32[1024]{0:T(1024)S(1)} fusion(bf16[1024,1408]{1,0:T(8,128)(2,1)} %all-gather.5.cloned.1.call-done), kind=kLoop, calls=%fused_computation.3 | loop fusion | flops 2882560 | bytes 2887680 | tf_op jit(solution)/shard_map/reduce_sum | solution.py:12
  65.4 0.3 copy-done.1
  65.6 0.9 fusion.4
  66.6 3.1 %fusion.27 = bf16[1024,528]{0,1:T(8,128)(2,1)} fusion(bf16[1408,528]{0,1:T(8,128)(2,1)S(1)} %bitcast.56, bf16[1024,1408]{1,0:T(8,128)(2,1)S(1)} %copy-done.1, f32[1408]{0:T(1024)S(1)} %copy-done.7, f32[1408]{0:T(1024)S(1)} %copy-done.8, f32[1024]{0:T(1024)S(1)} %add_rsqrt_fusion, f32[1024]{0:T(1024)S(1)} %broadcast_multiply_fusion), kind=kOutput, calls=%fused_computation.35 | convolution fusion | flops 1531723776 | bytes 5471232 | tf_op jit(solution)/shard_map/dot_general | solution.py:72
  69.7 4.8 %fusion.82 = (f32[2,512]{1,0:T(2,128)S(1)}, f32[2,512,1024]{2,1,0:T(8,128)}) fusion(pred[512,1024]{1,0:T(8,128)(4,1)S(1)} %get-tuple-element.5, bf16[1024,2,264]{0,2,1:T(8,128)(2,1)} %bitcast.67), kind=kOutput, calls=%fused_computation.86 | convolution fusion | flops 188744704 | bytes 5263360 | tf_op jit(solution)/shard_map/sub | solution.py:41
  74.5 4.8 %fusion.73 = (f32[2,512]{1,0:T(2,128)S(1)}, f32[2,512,1024]{2,1,0:T(8,128)}) fusion(pred[512,1024]{1,0:T(8,128)(4,1)S(1)} %get-tuple-element.6, bf16[1024,2,264]{0,2,1:T(8,128)(2,1)} %bitcast.68), kind=kOutput, calls=%fused_computation.85 | convolution fusion | flops 188744704 | bytes 5263360 | tf_op jit(solution)/shard_map/sub | solution.py:41
  79.3 3.2 %fusion.33 = bf16[512,2,88]{0,2,1:T(8,128)(2,1)S(1)} fusion(f32[2,512,1024]{2,1,0:T(8,128)} %get-tuple-element.12, f32[2,512]{1,0:T(2,128)S(1)} %get-tuple-element.11, bf16[1024,2,264]{0,2,1:T(8,128)(2,1)S(1)} %bitcast.69), kind=kOutput, calls=%fused_computation.41 | convolution fusion | flops 186736640 | bytes 4739072 | tf_op jit(solution)/shard_map/hqk,khd->qhd/dot_general | solution.py:43
  82.5 0.3 copy-done.11
  82.8 0.9 fusion.34
  83.7 0.0 copy-start.4
  83.7 0.0 copy-start.5
  83.7 0.1 copy.18
  83.9 5.6 %all-to-all-done.1 = bf16[8,2,88,1408]{3,2,1,0:T(8,128)(2,1)} async-done(((bf16[8,2,88,1408]{3,2,1,0:T(8,128)(2,1)}), bf16[8,2,88,1408]{3,2,1,0:T(8,128)(2,1)}, u32[]{:S(2)}, u32[]{:S(2)}) %all-to-all-start.1) | async-done | bytes 3964960 | tf_op jit(solution)/shard_map/all_to_all | solution.py:67
  89.5 11.0 %all_to_all.20 = bf16[8,128,176]{1,2,0:T(8,128)(2,1)S(1)} all-to-all(bf16[8,128,176]{1,2,0:T(8,128)(2,1)S(1)} %copy.14), channel_id=1, replica_groups=mesh['y'=4,'z'=16,'x'=4,'core'=2] {'x','core'}, dimensions={0} | all-to-all | bytes 720896 | tf_op jit(solution)/shard_map/all_to_all | solution.py:80
  100.5 3.1 %fusion.91 = (f32[128]{0:T(128)S(1)}, f32[128,1408]{1,0:T(8,128)S(1)}) fusion(bf16[8,128,176]{1,2,0:T(8,128)(2,1)S(1)} %all_to_all.20, bf16[8,176,1408]{2,1,0:T(8,128)(2,1)} %bitcast.10, bf16[128,1408]{1,0:T(8,128)(2,1)S(1)} %copy-done.2), kind=kOutput, calls=%fused_computation.87 | convolution fusion | flops 508411776 | bytes 5407232 | tf_op jit(solution)/shard_map/sqd,sdo->qo/dot_general | solution.py:82
  103.5 0.2 multiply_reduce_fusion
  103.8 0.2 add_convert_fusion
  104.0 0.2 broadcast_in_dim.65
  104.3 0.0 copy-start.3
  104.3 0.0 copy-start.9
  104.3 1.9 broadcast_in_dim.66
  106.2 4.6 %all-to-all-start.2 = ((bf16[8,32,5632]{2,1,0:T(8,128)(2,1)}), bf16[8,32,5632]{2,1,0:T(8,128)(2,1)}, u32[]{:S(2)}, u32[]{:S(2)}) async-start(bf16[8,32,5632]{2,1,0:T(8,128)(2,1)} %broadcast_in_dim.66), calls=%async_computation.2 | async-start | bytes 5767168 | tf_op jit(solution)/shard_map/all_to_all | solution.py:87
  110.8 0.6 reduce-window.6
  111.4 0.2 slice_reduce_fusion
  111.7 0.1 fusion.67
  111.8 34.5 %all-to-all-done.2 = bf16[8,32,5632]{2,1,0:T(8,128)(2,1)} async-done(((bf16[8,32,5632]{2,1,0:T(8,128)(2,1)}), bf16[8,32,5632]{2,1,0:T(8,128)(2,1)}, u32[]{:S(2)}, u32[]{:S(2)}) %all-to-all-start.2) | async-done | bytes 2883616 | tf_op jit(solution)/shard_map/all_to_all | solution.py:87
  146.2 4.0 %all-gather.7.cloned.1.call-done = bf16[4,1408,448]{2,1,0:T(8,128)(2,1)} async-done(((bf16[4,88,448]{2,1,0:T(8,128)(2,1)}), bf16[4,1408,448]{2,1,0:T(8,128)(2,1)}) %all-gather.7.cloned.1.call-update) | async-done | bytes 5046288 | tf_op jit(solution)/shard_map/all_gather | solution.py:64
  150.2 5.5 %convolution_convert_fusion = bf16[512,448]{0,1:T(8,128)(2,1)S(1)} fusion(bf16[256,5632]{1,0:T(8,128)(2,1)} %bitcast.12, bf16[5632,448]{1,0:T(8,128)(2,1)} %bitcast.66, f32[448]{0:T(512)S(1)} %copy-done.9, s32[256]{0:T(256)S(1)} %multiply_add_fusion), kind=kOutput, calls=%fused_computation.36 | convolution fusion | flops 1409875968 | bytes 8391424 | tf_op jit(solution)/shard_map/dot_general | solution.py:102
  155.7 0.2 copy.15
  155.9 42.8 %all_to_all.21 = bf16[64,8,448]{2,1,0:T(8,128)(2,1)S(1)} all-to-all(bf16[64,8,448]{2,1,0:T(8,128)(2,1)S(1)} %bitcast.57), channel_id=1, replica_groups=mesh['y'=4,'z'=16,'x'=4,'core'=2] {'y','z'}, dimensions={0} | all-to-all | bytes 917504 | tf_op jit(solution)/shard_map/all_to_all | solution.py:106
  198.7 1.0 copy.16
  (27 shorter events, 0.2 us)
Async XLA Ops:
  6.5 60.0 %copy-start = (bf16[1408,2,264]{0,2,1:T(8,128)(2,1)S(1)}, bf16[1408,2,264]{0,2,1:T(8,128)(2,1)}, u32[]{:S(2)}) copy-start(bf16[1408,2,264]{0,2,1:T(8,128)(2,1)} %param.14) | copy-start | bytes 4460548
  6.5 56.4 %all-gather.5.cloned.1.call-start = ((), (), s32[]{:S(2)}) async-start(), calls=%async_computation.4 | async-start | bytes 3244032 | tf_op jit(solution)/shard_map/all_gather | solution.py:65
  7.3 143.0 %all-gather.7.cloned.1.call-start = ((), (), s32[]{:S(2)}) async-start(), calls=%async_computation.5 | async-start | bytes 6127616 | tf_op jit(solution)/shard_map/all_gather | solution.py:64
  28.2 4.7 %copy-start.6 = (s32[1,256]{1,0:T(1,128)S(1)}, s32[1,256]{1,0:T(1,128)}, u32[]{:S(2)}) copy-start(s32[1,256]{1,0:T(1,128)} %param.20) | copy-start | bytes 3076
  28.2 61.2 %all-to-all-start.1 = ((bf16[8,2,88,1408]{3,2,1,0:T(8,128)(2,1)}), bf16[8,2,88,1408]{3,2,1,0:T(8,128)(2,1)}, u32[]{:S(2)}, u32[]{:S(2)}) async-start(bf16[8,2,88,1408]{3,2,1,0:T(8,128)(2,1)} %broadcast_in_dim.64), calls=%async_computation.1 | async-start | bytes 7929856 | tf_op jit(solution)/shard_map/all_to_all | solution.py:67
  32.9 33.6 %copy-start.7 = (f32[1408]{0:T(1024)S(1)}, f32[1408]{0:T(1024)}, u32[]{:S(2)}) copy-start(f32[1408]{0:T(1024)} %param.13) | copy-start | bytes 16900
  32.9 33.6 %copy-start.8 = (f32[1408]{0:T(1024)S(1)}, f32[1408]{0:T(1024)}, u32[]{:S(2)}) copy-start(f32[1408]{0:T(1024)} %param.12) | copy-start | bytes 16900
  63.0 2.7 %copy-start.1 = (bf16[1024,1408]{1,0:T(8,128)(2,1)S(1)}, bf16[1024,1408]{1,0:T(8,128)(2,1)}, u32[]{:S(2)}) copy-start(bf16[1024,1408]{1,0:T(8,128)(2,1)} %all-gather.5.cloned.1.call-done) | copy-start | bytes 8650756
  74.5 4.8 %copy-start.10 = (bf16[1024,528]{0,1:T(8,128)(2,1)S(1)}, bf16[1024,528]{0,1:T(8,128)(2,1)}, u32[]{:S(2)}) copy-start(bf16[1024,528]{0,1:T(8,128)(2,1)} %fusion.27) | copy-start | bytes 3244036
  79.3 3.4 %copy-start.11 = (f32[2,512,1024]{2,1,0:T(8,128)S(1)}, f32[2,512,1024]{2,1,0:T(8,128)}, u32[]{:S(2)}) copy-start(f32[2,512,1024]{2,1,0:T(8,128)} %get-tuple-element.10) | copy-start | bytes 12582916
  82.8 17.7 %copy-start.2 = (bf16[128,1408]{1,0:T(8,128)(2,1)S(1)}, bf16[128,1408]{1,0:T(8,128)(2,1)}, u32[]{:S(2)}) copy-start(bf16[128,1408]{1,0:T(8,128)(2,1)} %param.11) | copy-start | bytes 1081348
  83.7 20.1 %copy-start.4 = (f32[1408]{0:T(1024)S(1)}, f32[1408]{0:T(1024)}, u32[]{:S(2)}) copy-start(f32[1408]{0:T(1024)} %param.17) | copy-start | bytes 16900
  83.7 20.1 %copy-start.5 = (f32[1408]{0:T(1024)S(1)}, f32[1408]{0:T(1024)}, u32[]{:S(2)}) copy-start(f32[1408]{0:T(1024)} %param.16) | copy-start | bytes 16900
  104.3 6.5 %copy-start.3 = (s32[256,1]{0,1:T(1,128)S(1)}, s32[256,1]{0,1:T(1,128)}, u32[]{:S(2)}) copy-start(s32[256,1]{0,1:T(1,128)} %param.21) | copy-start | bytes 3076
  104.3 46.0 %copy-start.9 = (f32[448]{0:T(512)S(1)}, f32[448]{0:T(512)}, u32[]{:S(2)}) copy-start(f32[448]{0:T(512)} %param.19) | copy-start | bytes 5380
  106.2 40.1 %all-to-all-start.2 = ((bf16[8,32,5632]{2,1,0:T(8,128)(2,1)}), bf16[8,32,5632]{2,1,0:T(8,128)(2,1)}, u32[]{:S(2)}, u32[]{:S(2)}) async-start(bf16[8,32,5632]{2,1,0:T(8,128)(2,1)} %broadcast_in_dim.66), calls=%async_computation.2 | async-start | bytes 5767168 | tf_op jit(solution)/shard_map/all_to_all | solution.py:87
Sparse Core Ops, SparseCore 0:
  9.5 53.4 all-gather.4
  65.0 85.1 all-gather.6

commit v7 on v6

--- a/solution.py
+++ b/solution.py
@@ -64,8 +64,9 @@
     w_proj_all = lax.all_gather(w_y, "z", axis=1).reshape(-1, w_proj.shape[1])
     gathered = lax.all_gather(tokens, TP, axis=0, tiled=True)
     tp_n = lax.axis_size("x") * lax.axis_size("core")
-    w_out_all = lax.all_to_all(jnp.broadcast_to(w_out[None], (tp_n,) + w_out.shape), TP, 0, 0, tiled=True)
-    w_out_all = w_out_all.reshape((-1,) + w_out.shape[1:])
+    nx, nc = lax.axis_size("x"), lax.axis_size("core")
+    w_out_x = lax.all_to_all(jnp.broadcast_to(w_out[None], (nx,) + w_out.shape), "x", 0, 0, tiled=True)
+    w_out_all = lax.all_to_all(jnp.broadcast_to(w_out_x[None], (nc,) + w_out_x.shape), "core", 0, 0, tiled=True)
     row_count = gathered.shape[0]
     normed = layer_norm(gathered, ln1_gain, ln1_shift).astype(jnp.bfloat16)
     heads_here = w_qkv.shape[1]
@@ -78,8 +79,9 @@
     tp_count = lax.axis_size("x") * lax.axis_size("core")
     local_rows = tokens.shape[0]
     context_mine = lax.all_to_all(context.reshape(tp_count, local_rows, -1), TP, 0, 0, tiled=True)
-    out_heads = w_out_all.reshape(tp_count, -1, w_out_all.shape[2])
-    attn = jnp.einsum("sqd,sdo->qo", context_mine, out_heads, preferred_element_type=jnp.float32)
+    out_heads = w_out_all.reshape(nc, nx, -1, w_out_all.shape[-1])
+    context_xc = context_mine.reshape(nx, nc, local_rows, -1)
+    attn = jnp.einsum("xcqd,cxdo->qo", context_xc, out_heads, preferred_element_type=jnp.float32)
     hidden = (tokens.astype(jnp.float32) + attn).astype(jnp.bfloat16)
     normed_two = layer_norm(hidden, ln2_gain, ln2_shift).astype(jnp.bfloat16)
     merged_mine = normed_two.reshape(local_rows // 4, -1)

time: 207 us -> 196 us (0.947)
  waiting for transfers between devices: 73.5 us -> 54 us
  starting transfers between devices: 9.32 us -> 14.4 us
  local copies, waits for them, and re-layouts: 7.99 us -> 11 us
    all_gather x1, waiting for transfers between devices: 28.7 us -> 0.29 us  [shards(): gathered = lax.all_gather(tokens, TP, axis=0, tiled=True)]
    all_to_all x1 -> x2, starting transfers between devices: 4.68 us -> 9.8 us  [the longest x1 5.5 us: shards(): lax.all_to_all(jnp.broadcast_to(w_out_x[None], (nc,) + w_out_x.shape), 'c...]
    all_gather x1, waiting for transfers between devices: 3.99 us -> 8.98 us  [shards(): w_proj_all = lax.all_gather(w_y, 'z', axis=1).reshape(-1, w_proj.shape[1])]
    all_to_all x1 -> x2, waiting for transfers between devices: 5.62 us -> 9.56 us  [the longest x1 9.55 us: shards(): lax.all_to_all(jnp.broadcast_to(w_out[None], (nx,) + w_out.shape), 'x', 0...]
    all_to_all x1, blocking collectives: 11 us -> 13.1 us  [shards(): lax.all_to_all(context.reshape(tp_count, local_rows, -1), TP, 0, 0, tiled...]
    broadcast_in_dim x1 -> x2, local copies, waits for them, and re-layouts: 3.22 us -> 4.7 us  [the longest x1 2.5 us: shards(): jnp.broadcast_to(w_out[None], (nx,) + w_out.shape)]
  transfers between devices with their start and end apart: 4 -> 5, of which waited for: 4 -> 4; matrix products, arithmetic and copies ran while one was open for 15% -> 18% of each run, Pallas kernels for 0% -> 0%
where the time goes in v7:
time: 196 us
  blocking collectives  71 us (36%)
  waiting for transfers between devices  54 us (28%)
  matrix products  25.4 us (13%)
  starting transfers between devices  14.4 us (7%)
  between operations  13.6 us (7%)
  local copies, waits for them, and re-layouts  11 us (6%)
  other arithmetic  6.19 us (3%)
    all_to_all x1, blocking collectives, shards(): lax.all_to_all(outgoing, DP, split_axis=0, concat_axis=0, tiled=True)  41 us
    all_to_all x1, waiting for transfers between devices, shards(): lax.all_to_all(copies, TP, 0, 0, tiled=True)  34.5 us
    all_gather x1, blocking collectives, shards(): w_y = lax.all_gather(w_proj, 'y', axis=0)  16.9 us
    all_to_all x1, blocking collectives, shards(): lax.all_to_all(context.reshape(tp_count, local_rows, -1), TP, 0, 0, tiled...  13.1 us
    sub x2, matrix products, attend(): exponent = jnp.exp(scores - row_max)  9.66 us
    all_to_all x1, waiting for transfers between devices, shards(): lax.all_to_all(jnp.broadcast_to(w_out[None], (nx,) + w_out.shape), 'x', 0...  9.55 us
    all_gather x1, waiting for transfers between devices, shards(): w_proj_all = lax.all_gather(w_y, 'z', axis=1).reshape(-1, w_proj.shape[1])  8.98 us
    all_to_all x1, starting transfers between devices, shards(): lax.all_to_all(jnp.broadcast_to(w_out_x[None], (nc,) + w_out_x.shape), 'c...  5.5 us
  transfers between devices with their start and end apart: 5, of which 4 were waited for; matrix products, arithmetic and copies ran while one was open for 18% of the time, Pallas kernels for 0%

profile of v7, /device:TPU:8, one launch (start us, length us, event | category | flops | bytes accessed | tf_op | source)
XLA Modules:
  0.0 195.7 jit_solution(4552268485156815972)
XLA Ops:
  6.5 0.7 all-gather.5.cloned.1.call-update
  7.3 2.5 %broadcast_in_dim.38 = bf16[4,2,88,1408]{3,2,1,0:T(8,128)(2,1)} broadcast(bf16[2,88,1408]{2,1,0:T(8,128)(2,1)} %param.15), dimensions={1,2,3} | broadcast | bytes 2478080 | tf_op jit(solution)/shard_map/broadcast_in_dim | solution.py:68
  9.8 4.3 %all-to-all-start.1 = ((bf16[4,2,88,1408]{3,2,1,0:T(8,128)(2,1)}), bf16[4,2,88,1408]{3,2,1,0:T(8,128)(2,1)S(1)}, u32[]{:S(2)}, u32[]{:S(2)}) async-start(bf16[4,2,88,1408]{3,2,1,0:T(8,128)(2,1)} %broadcast_in_dim.38), calls=%async_computation.1 | async-start | bytes 3964928 | tf_op jit(solution)/shard_map/all_to_all | solution.py:68
  14.1 16.9 %all-gather = bf16[352,448]{1,0:T(8,128)(2,1)} all-gather(bf16[88,448]{1,0:T(8,128)(2,1)} %param.18), channel_id=2, replica_groups=mesh['y'=4,'z'=16,'x'=4,'core'=2] {'y'}, dimensions={0}, use_global_device_ids=true | all-gather | bytes 394240 | tf_op jit(solution)/shard_map/all_gather | solution.py:63
  30.9 0.0 all-gather.7.cloned.1.call-update
  31.0 0.1 broadcast_in_dim.32
  31.1 0.1 eq.84
  31.2 0.1 broadcast_in_dim.36
  31.3 0.1 eq.89
  31.4 0.8 broadcast_in_dim.33
  32.1 1.0 eq.86
  33.2 1.6 broadcast_compare_fusion.1
  34.8 9.6 %all-to-all-done.1 = bf16[4,2,88,1408]{3,2,1,0:T(8,128)(2,1)S(1)} async-done(((bf16[4,2,88,1408]{3,2,1,0:T(8,128)(2,1)}), bf16[4,2,88,1408]{3,2,1,0:T(8,128)(2,1)S(1)}, u32[]{:S(2)}, u32[]{:S(2)}) %all-to-all-start.1) | async-done | bytes 1982496 | tf_op jit(solution)/shard_map/all_to_all | solution.py:68
  44.3 2.2 %broadcast_in_dim.39 = bf16[2,4,2,88,1408]{4,3,2,1,0:T(8,128)(2,1)} broadcast(bf16[4,2,88,1408]{3,2,1,0:T(8,128)(2,1)S(1)} %all-to-all-done.1), dimensions={1,2,3,4} | broadcast | bytes 5947392 | tf_op jit(solution)/shard_map/broadcast_in_dim | solution.py:69
  46.5 5.5 %all-to-all-start.2 = ((bf16[2,4,2,88,1408]{4,3,2,1,0:T(8,128)(2,1)}), bf16[2,4,2,88,1408]{4,3,2,1,0:T(8,128)(2,1)}, u32[]{:S(2)}, u32[]{:S(2)}) async-start(bf16[2,4,2,88,1408]{4,3,2,1,0:T(8,128)(2,1)} %broadcast_in_dim.39), calls=%async_computation.2 | async-start | bytes 7929856 | tf_op jit(solution)/shard_map/all_to_all | solution.py:69
  52.1 0.0 copy-start.9
  52.1 0.3 all-gather.5.cloned.1.call-done
  52.4 2.4 %convert_reduce_fusion = f32[1024]{0:T(1024)S(1)} fusion(bf16[1024,1408]{1,0:T(8,128)(2,1)} %all-gather.5.cloned.1.call-done), kind=kLoop, calls=%fused_computation.3 | loop fusion | flops 2882560 | bytes 2887680 | tf_op jit(solution)/shard_map/reduce_sum | solution.py:12
  54.8 0.3 copy-done.1
  55.0 0.9 fusion.4
  56.0 3.1 %fusion.27 = bf16[1024,528]{0,1:T(8,128)(2,1)} fusion(bf16[1408,528]{0,1:T(8,128)(2,1)S(1)} %bitcast.58, bf16[1024,1408]{1,0:T(8,128)(2,1)S(1)} %copy-done.1, f32[1408]{0:T(1024)S(1)} %copy-done.9, f32[1408]{0:T(1024)S(1)} %copy-done.10, f32[1024]{0:T(1024)S(1)} %add_rsqrt_fusion, f32[1024]{0:T(1024)S(1)} %broadcast_multiply_fusion), kind=kOutput, calls=%fused_computation.35 | convolution fusion | flops 1531723776 | bytes 5471232 | tf_op jit(solution)/shard_map/dot_general | solution.py:73
  59.1 4.8 %fusion.83 = (f32[2,512]{1,0:T(2,128)S(1)}, f32[2,512,1024]{2,1,0:T(8,128)}) fusion(pred[512,1024]{1,0:T(8,128)(4,1)S(1)} %copy-done.4, bf16[1024,2,264]{0,2,1:T(8,128)(2,1)} %bitcast.70), kind=kOutput, calls=%fused_computation.87 | convolution fusion | flops 188744704 | bytes 5263360 | tf_op jit(solution)/shard_map/sub | solution.py:41
  63.9 4.9 %fusion.74 = (f32[2,512]{1,0:T(2,128)S(1)}, f32[2,512,1024]{2,1,0:T(8,128)}) fusion(pred[512,1024]{1,0:T(8,128)(4,1)S(1)} %copy-done.3, bf16[1024,2,264]{0,2,1:T(8,128)(2,1)} %bitcast.71), kind=kOutput, calls=%fused_computation.86 | convolution fusion | flops 188744704 | bytes 5263360 | tf_op jit(solution)/shard_map/sub | solution.py:41
  68.8 3.2 %fusion.33 = bf16[512,2,88]{0,2,1:T(8,128)(2,1)S(1)} fusion(f32[2,512,1024]{2,1,0:T(8,128)} %get-tuple-element.12, f32[2,512]{1,0:T(2,128)S(1)} %get-tuple-element.11, bf16[1024,2,264]{0,2,1:T(8,128)(2,1)S(1)} %bitcast.72), kind=kOutput, calls=%fused_computation.41 | convolution fusion | flops 186736640 | bytes 4739072 | tf_op jit(solution)/shard_map/hqk,khd->qhd/dot_general | solution.py:43
  72.0 0.3 copy-done.13
  72.3 0.9 fusion.34
  73.2 0.0 copy-start.6
  73.2 0.0 copy-start.7
  73.2 0.1 copy.19
  73.3 0.0 all-to-all-done.2
  73.3 13.1 %all_to_all.25 = bf16[8,128,176]{1,2,0:T(8,128)(2,1)S(1)} all-to-all(bf16[8,128,176]{1,2,0:T(8,128)(2,1)S(1)} %copy.13), channel_id=1, replica_groups=mesh['y'=4,'z'=16,'x'=4,'core'=2] {'x','core'}, dimensions={0} | all-to-all | bytes 720896 | tf_op jit(solution)/shard_map/all_to_all | solution.py:81
  86.5 3.1 %fusion.92 = (f32[128]{0:T(128)S(1)}, f32[128,1408]{1,0:T(8,128)S(1)}) fusion(bf16[2,4,176,1408]{3,2,1,0:T(8,128)(2,1)} %bitcast.11, bf16[4,2,128,176]{2,3,1,0:T(8,128)(2,1)S(1)} %bitcast.64, bf16[128,1408]{1,0:T(8,128)(2,1)S(1)} %copy-done.2), kind=kOutput, calls=%fused_computation.88 | convolution fusion | flops 508411776 | bytes 5407232 | tf_op jit(solution)/shard_map/xcqd,cxdo->qo/dot_general | solution.py:84
  89.5 0.2 multiply_reduce_fusion
  89.8 0.2 add_convert_fusion
  90.0 0.2 broadcast_in_dim.72
  90.2 0.0 copy-start.5
  90.2 0.0 copy-start.11
  90.2 1.9 broadcast_in_dim.73
  92.1 4.6 %all-to-all-start.3 = ((bf16[8,32,5632]{2,1,0:T(8,128)(2,1)}), bf16[8,32,5632]{2,1,0:T(8,128)(2,1)}, u32[]{:S(2)}, u32[]{:S(2)}) async-start(bf16[8,32,5632]{2,1,0:T(8,128)(2,1)} %broadcast_in_dim.73), calls=%async_computation.3 | async-start | bytes 5767168 | tf_op jit(solution)/shard_map/all_to_all | solution.py:89
  96.8 0.6 reduce-window.6
  97.4 0.2 slice_reduce_fusion
  97.6 0.1 fusion.68
  97.7 34.5 %all-to-all-done.3 = bf16[8,32,5632]{2,1,0:T(8,128)(2,1)} async-done(((bf16[8,32,5632]{2,1,0:T(8,128)(2,1)}), bf16[8,32,5632]{2,1,0:T(8,128)(2,1)}, u32[]{:S(2)}, u32[]{:S(2)}) %all-to-all-start.3) | async-done | bytes 2883616 | tf_op jit(solution)/shard_map/all_to_all | solution.py:89
  132.2 9.0 %all-gather.7.cloned.1.call-done = bf16[4,1408,448]{2,1,0:T(8,128)(2,1)} async-done(((bf16[4,88,448]{2,1,0:T(8,128)(2,1)}), bf16[4,1408,448]{2,1,0:T(8,128)(2,1)}) %all-gather.7.cloned.1.call-update) | async-done | bytes 5046288 | tf_op jit(solution)/shard_map/all_gather | solution.py:64
  141.2 5.5 %convolution_convert_fusion = bf16[512,448]{0,1:T(8,128)(2,1)S(1)} fusion(bf16[256,5632]{1,0:T(8,128)(2,1)} %bitcast.14, bf16[5632,448]{1,0:T(8,128)(2,1)} %bitcast.69, f32[448]{0:T(512)S(1)} %copy-done.11, s32[256]{0:T(256)S(1)} %multiply_add_fusion), kind=kOutput, calls=%fused_computation.36 | convolution fusion | flops 1409875968 | bytes 8391424 | tf_op jit(solution)/shard_map/dot_general | solution.py:104
  146.6 0.2 copy.15
  146.9 41.0 %all_to_all.26 = bf16[64,8,448]{2,1,0:T(8,128)(2,1)S(1)} all-to-all(bf16[64,8,448]{2,1,0:T(8,128)(2,1)S(1)} %bitcast.59), channel_id=1, replica_groups=mesh['y'=4,'z'=16,'x'=4,'core'=2] {'y','z'}, dimensions={0} | all-to-all | bytes 917504 | tf_op jit(solution)/shard_map/all_to_all | solution.py:108
  187.9 1.0 copy.16
  (34 shorter events, 0.2 us)
Async XLA Ops:
  6.5 49.4 %copy-start = (bf16[1408,2,264]{0,2,1:T(8,128)(2,1)S(1)}, bf16[1408,2,264]{0,2,1:T(8,128)(2,1)}, u32[]{:S(2)}) copy-start(bf16[1408,2,264]{0,2,1:T(8,128)(2,1)} %param.14) | copy-start | bytes 4460548
  6.5 24.4 %copy-start.8 = (s32[1,256]{1,0:T(1,128)S(1)}, s32[1,256]{1,0:T(1,128)}, u32[]{:S(2)}) copy-start(s32[1,256]{1,0:T(1,128)} %param.20) | copy-start | bytes 3076
  6.5 45.8 %all-gather.5.cloned.1.call-start = ((), (), s32[]{:S(2)}) async-start(), calls=%async_computation.5 | async-start | bytes 3244032 | tf_op jit(solution)/shard_map/all_gather | solution.py:65
  9.8 34.6 %all-to-all-start.1 = ((bf16[4,2,88,1408]{3,2,1,0:T(8,128)(2,1)}), bf16[4,2,88,1408]{3,2,1,0:T(8,128)(2,1)S(1)}, u32[]{:S(2)}, u32[]{:S(2)}) async-start(bf16[4,2,88,1408]{3,2,1,0:T(8,128)(2,1)} %broadcast_in_dim.38), calls=%async_computation.1 | async-start | bytes 3964928 | tf_op jit(solution)/shard_map/all_to_all | solution.py:68
  14.1 127.1 %all-gather.7.cloned.1.call-start = ((), (), s32[]{:S(2)}) async-start(), calls=%async_computation.6 | async-start | bytes 6127616 | tf_op jit(solution)/shard_map/all_gather | solution.py:64
  46.5 26.8 %all-to-all-start.2 = ((bf16[2,4,2,88,1408]{4,3,2,1,0:T(8,128)(2,1)}), bf16[2,4,2,88,1408]{4,3,2,1,0:T(8,128)(2,1)}, u32[]{:S(2)}, u32[]{:S(2)}) async-start(bf16[2,4,2,88,1408]{4,3,2,1,0:T(8,128)(2,1)} %broadcast_in_dim.39), calls=%async_computation.2 | async-start | bytes 7929856 | tf_op jit(solution)/shard_map/all_to_all | solution.py:69
  52.1 3.9 %copy-start.9 = (f32[1408]{0:T(1024)S(1)}, f32[1408]{0:T(1024)}, u32[]{:S(2)}) copy-start(f32[1408]{0:T(1024)} %param.13) | copy-start | bytes 16900
  52.4 2.7 %copy-start.1 = (bf16[1024,1408]{1,0:T(8,128)(2,1)S(1)}, bf16[1024,1408]{1,0:T(8,128)(2,1)}, u32[]{:S(2)}) copy-start(bf16[1024,1408]{1,0:T(8,128)(2,1)} %all-gather.5.cloned.1.call-done) | copy-start | bytes 8650756
  52.4 3.6 %copy-start.10 = (f32[1408]{0:T(1024)S(1)}, f32[1408]{0:T(1024)}, u32[]{:S(2)}) copy-start(f32[1408]{0:T(1024)} %param.12) | copy-start | bytes 16900
  56.0 3.2 %copy-start.4 = (pred[512,1024]{1,0:T(8,128)(4,1)S(1)}, pred[512,1024]{1,0:T(8,128)(4,1)}, u32[]{:S(2)}) copy-start(pred[512,1024]{1,0:T(8,128)(4,1)} %get-tuple-element.5) | copy-start | bytes 1572868
  59.1 4.8 %copy-start.3 = (pred[512,1024]{1,0:T(8,128)(4,1)S(1)}, pred[512,1024]{1,0:T(8,128)(4,1)}, u32[]{:S(2)}) copy-start(pred[512,1024]{1,0:T(8,128)(4,1)} %get-tuple-element.6) | copy-start | bytes 1572868
  63.9 4.9 %copy-start.12 = (bf16[1024,528]{0,1:T(8,128)(2,1)S(1)}, bf16[1024,528]{0,1:T(8,128)(2,1)}, u32[]{:S(2)}) copy-start(bf16[1024,528]{0,1:T(8,128)(2,1)} %fusion.27) | copy-start | bytes 3244036
  68.8 3.4 %copy-start.13 = (f32[2,512,1024]{2,1,0:T(8,128)S(1)}, f32[2,512,1024]{2,1,0:T(8,128)}, u32[]{:S(2)}) copy-start(f32[2,512,1024]{2,1,0:T(8,128)} %get-tuple-element.10) | copy-start | bytes 12582916
  72.3 14.2 %copy-start.2 = (bf16[128,1408]{1,0:T(8,128)(2,1)S(1)}, bf16[128,1408]{1,0:T(8,128)(2,1)}, u32[]{:S(2)}) copy-start(bf16[128,1408]{1,0:T(8,128)(2,1)} %param.11) | copy-start | bytes 1081348
  73.2 16.6 %copy-start.6 = (f32[1408]{0:T(1024)S(1)}, f32[1408]{0:T(1024)}, u32[]{:S(2)}) copy-start(f32[1408]{0:T(1024)} %param.17) | copy-start | bytes 16900
  73.2 16.6 %copy-start.7 = (f32[1408]{0:T(1024)S(1)}, f32[1408]{0:T(1024)}, u32[]{:S(2)}) copy-start(f32[1408]{0:T(1024)} %param.16) | copy-start | bytes 16900
  90.2 6.5 %copy-start.5 = (s32[256,1]{0,1:T(1,128)S(1)}, s32[256,1]{0,1:T(1,128)}, u32[]{:S(2)}) copy-start(s32[256,1]{0,1:T(1,128)} %param.21) | copy-start | bytes 3076
  90.2 51.0 %copy-start.11 = (f32[448]{0:T(512)S(1)}, f32[448]{0:T(512)}, u32[]{:S(2)}) copy-start(f32[448]{0:T(512)} %param.19) | copy-start | bytes 5380
  92.1 40.1 %all-to-all-start.3 = ((bf16[8,32,5632]{2,1,0:T(8,128)(2,1)}), bf16[8,32,5632]{2,1,0:T(8,128)(2,1)}, u32[]{:S(2)}, u32[]{:S(2)}) async-start(bf16[8,32,5632]{2,1,0:T(8,128)(2,1)} %broadcast_in_dim.73), calls=%async_computation.3 | async-start | bytes 5767168 | tf_op jit(solution)/shard_map/all_to_all | solution.py:89
Sparse Core Ops, SparseCore 0:
  9.5 42.8 all-gather.4
  54.4 86.6 all-gather.6

commit v8 on v7

--- a/solution.py
+++ b/solution.py
@@ -85,8 +85,10 @@
     hidden = (tokens.astype(jnp.float32) + attn).astype(jnp.bfloat16)
     normed_two = layer_norm(hidden, ln2_gain, ln2_shift).astype(jnp.bfloat16)
     merged_mine = normed_two.reshape(local_rows // 4, -1)
-    copies = jnp.broadcast_to(merged_mine[None], (tp_count,) + merged_mine.shape)
-    merged = lax.all_to_all(copies, TP, 0, 0, tiled=True).reshape(-1, merged_mine.shape[1])
+    copies = jnp.broadcast_to(merged_mine[None], (nx,) + merged_mine.shape)
+    merged_x = lax.all_to_all(copies, "x", 0, 0, tiled=True)
+    pair = jnp.broadcast_to(merged_x[None], (nc,) + merged_x.shape)
+    merged = lax.all_to_all(pair, "core", 0, 0, tiled=True).reshape(-1, merged_mine.shape[1])
     groups = merged.shape[0]
     summed = jnp.dot(
         merged, w_proj_all, preferred_element_type=jnp.float32
@@ -98,6 +100,7 @@
     position = jnp.sum(earlier * onehot, axis=1)
     capacity = 2 * groups // dp_count
     slot_index = dests * capacity + position
+    slot_index = slot_index.reshape(nx, nc, -1).transpose(1, 0, 2).reshape(-1)
     scatter_table = (
         slot_index[None, :] == jnp.arange(dp_count * capacity, dtype=jnp.int32)[:, None]
     ).astype(jnp.bfloat16)

time: 196 us -> 203 us (1.036)
  the two profiles are of different devices: /device:TPU:8 before, /device:TPU:14 now
where the time goes in v8:
time: 203 us
  blocking collectives  69.5 us (34%)
  waiting for transfers between devices  57.3 us (28%)
  matrix products  25.9 us (13%)
  starting transfers between devices  19.2 us (9%)
  between operations  13.6 us (7%)
  local copies, waits for them, and re-layouts  10.8 us (5%)
  other arithmetic  6.21 us (3%)
    all_to_all x1, blocking collectives, shards(): lax.all_to_all(outgoing, DP, split_axis=0, concat_axis=0, tiled=True)  37.9 us
    all_to_all x1, waiting for transfers between devices, shards(): lax.all_to_all(jnp.broadcast_to(w_out[None], (nx,) + w_out.shape), 'x', 0...  24.6 us
    all_to_all x1, waiting for transfers between devices, shards(): merged_x = lax.all_to_all(copies, 'x', 0, 0, tiled=True)  16.2 us
    all_gather x1, waiting for transfers between devices, shards(): w_proj_all = lax.all_gather(w_y, 'z', axis=1).reshape(-1, w_proj.shape[1])  15.8 us
    all_gather x1, blocking collectives, shards(): w_y = lax.all_gather(w_proj, 'y', axis=0)  13.6 us
    all_to_all x1, blocking collectives, shards(): lax.all_to_all(context.reshape(tp_count, local_rows, -1), TP, 0, 0, tiled...  11 us
    sub x2, matrix products, attend(): exponent = jnp.exp(scores - row_max)  9.67 us
    all_to_all x1, starting transfers between devices, shards(): lax.all_to_all(jnp.broadcast_to(w_out[None], (nx,) + w_out.shape), 'x', 0...  8.12 us
  transfers between devices with their start and end apart: 5, of which 3 were waited for; matrix products, arithmetic and copies ran while one was open for 17% of the time, Pallas kernels for 0%

profile of v8, /device:TPU:14, one launch (start us, length us, event | category | flops | bytes accessed | tf_op | source)
XLA Modules:
  0.0 202.6 jit_solution(15002426435357109432)
XLA Ops:
  6.5 0.7 all-gather.5.cloned.1.call-update
  7.3 0.0 all-gather.7.cloned.1.call-start
  7.3 13.6 %all-gather = bf16[352,448]{1,0:T(8,128)(2,1)} all-gather(bf16[88,448]{1,0:T(8,128)(2,1)} %param.18), channel_id=2, replica_groups=mesh['y'=4,'z'=16,'x'=4,'core'=2] {'y'}, dimensions={0}, use_global_device_ids=true | all-gather | bytes 394240 | tf_op jit(solution)/shard_map/all_gather | solution.py:63
  20.9 0.0 all-gather.7.cloned.1.call-update
  21.0 2.5 %broadcast_in_dim.40 = bf16[4,2,88,1408]{3,2,1,0:T(8,128)(2,1)} broadcast(bf16[2,88,1408]{2,1,0:T(8,128)(2,1)} %param.15), dimensions={1,2,3} | broadcast | bytes 2478080 | tf_op jit(solution)/shard_map/broadcast_in_dim | solution.py:68
  23.5 8.1 %all-to-all-start.1 = ((bf16[4,2,88,1408]{3,2,1,0:T(8,128)(2,1)}), bf16[4,2,88,1408]{3,2,1,0:T(8,128)(2,1)S(1)}, u32[]{:S(2)}, u32[]{:S(2)}) async-start(bf16[4,2,88,1408]{3,2,1,0:T(8,128)(2,1)} %broadcast_in_dim.40), calls=%async_computation.1 | async-start | bytes 3964928 | tf_op jit(solution)/shard_map/all_to_all | solution.py:68
  31.6 0.1 broadcast_in_dim.34
  31.7 0.1 eq.90
  31.8 0.1 broadcast_in_dim.38
  31.9 0.1 eq.95
  32.0 0.8 broadcast_in_dim.35
  32.7 1.0 eq.92
  33.8 1.6 broadcast_compare_fusion.1
  35.4 24.6 %all-to-all-done.1 = bf16[4,2,88,1408]{3,2,1,0:T(8,128)(2,1)S(1)} async-done(((bf16[4,2,88,1408]{3,2,1,0:T(8,128)(2,1)}), bf16[4,2,88,1408]{3,2,1,0:T(8,128)(2,1)S(1)}, u32[]{:S(2)}, u32[]{:S(2)}) %all-to-all-start.1) | async-done | bytes 1982496 | tf_op jit(solution)/shard_map/all_to_all | solution.py:68
  60.0 2.2 %broadcast_in_dim.41 = bf16[2,4,2,88,1408]{4,3,2,1,0:T(8,128)(2,1)} broadcast(bf16[4,2,88,1408]{3,2,1,0:T(8,128)(2,1)S(1)} %all-to-all-done.1), dimensions={1,2,3,4} | broadcast | bytes 5947392 | tf_op jit(solution)/shard_map/broadcast_in_dim | solution.py:69
  62.2 5.5 %all-to-all-start.2 = ((bf16[2,4,2,88,1408]{4,3,2,1,0:T(8,128)(2,1)}), bf16[2,4,2,88,1408]{4,3,2,1,0:T(8,128)(2,1)}, u32[]{:S(2)}, u32[]{:S(2)}) async-start(bf16[2,4,2,88,1408]{4,3,2,1,0:T(8,128)(2,1)} %broadcast_in_dim.41), calls=%async_computation.2 | async-start | bytes 7929856 | tf_op jit(solution)/shard_map/all_to_all | solution.py:69
  67.7 0.0 all-gather.5.cloned.1.call-done
  67.7 2.4 %convert_reduce_fusion = f32[1024]{0:T(1024)S(1)} fusion(bf16[1024,1408]{1,0:T(8,128)(2,1)} %all-gather.5.cloned.1.call-done), kind=kLoop, calls=%fused_computation.3 | loop fusion | flops 2882560 | bytes 2887680 | tf_op jit(solution)/shard_map/reduce_sum | solution.py:12
  70.2 0.2 copy-done.1
  70.4 0.9 fusion.4
  71.3 3.1 %fusion.27 = bf16[1024,528]{0,1:T(8,128)(2,1)} fusion(bf16[1408,528]{0,1:T(8,128)(2,1)S(1)} %bitcast.60, bf16[1024,1408]{1,0:T(8,128)(2,1)S(1)} %copy-done.1, f32[1408]{0:T(1024)S(1)} %copy-done.9, f32[1408]{0:T(1024)S(1)} %copy-done.10, f32[1024]{0:T(1024)S(1)} %add_rsqrt_fusion, f32[1024]{0:T(1024)S(1)} %broadcast_multiply_fusion), kind=kOutput, calls=%fused_computation.35 | convolution fusion | flops 1531723776 | bytes 5471232 | tf_op jit(solution)/shard_map/dot_general | solution.py:73
  74.5 4.8 %fusion.83 = (f32[2,512]{1,0:T(2,128)S(1)}, f32[2,512,1024]{2,1,0:T(8,128)}) fusion(pred[512,1024]{1,0:T(8,128)(4,1)S(1)} %copy-done.4, bf16[1024,2,264]{0,2,1:T(8,128)(2,1)} %bitcast.72), kind=kOutput, calls=%fused_computation.88 | convolution fusion | flops 188744704 | bytes 5263360 | tf_op jit(solution)/shard_map/sub | solution.py:41
  79.3 4.9 %fusion.74 = (f32[2,512]{1,0:T(2,128)S(1)}, f32[2,512,1024]{2,1,0:T(8,128)}) fusion(pred[512,1024]{1,0:T(8,128)(4,1)S(1)} %copy-done.3, bf16[1024,2,264]{0,2,1:T(8,128)(2,1)} %bitcast.73), kind=kOutput, calls=%fused_computation.87 | convolution fusion | flops 188744704 | bytes 5263360 | tf_op jit(solution)/shard_map/sub | solution.py:41
  84.2 3.2 %fusion.33 = bf16[512,2,88]{0,2,1:T(8,128)(2,1)S(1)} fusion(f32[2,512,1024]{2,1,0:T(8,128)} %get-tuple-element.12, f32[2,512]{1,0:T(2,128)S(1)} %get-tuple-element.11, bf16[1024,2,264]{0,2,1:T(8,128)(2,1)S(1)} %bitcast.74), kind=kOutput, calls=%fused_computation.41 | convolution fusion | flops 186736640 | bytes 4739072 | tf_op jit(solution)/shard_map/hqk,khd->qhd/dot_general | solution.py:43
  87.4 0.3 copy-done.13
  87.6 0.9 fusion.34
  88.5 0.1 copy.26
  88.7 11.0 %all_to_all.30 = bf16[8,128,176]{1,2,0:T(8,128)(2,1)S(1)} all-to-all(bf16[8,128,176]{1,2,0:T(8,128)(2,1)S(1)} %copy.20), channel_id=1, replica_groups=mesh['y'=4,'z'=16,'x'=4,'core'=2] {'x','core'}, dimensions={0} | all-to-all | bytes 720896 | tf_op jit(solution)/shard_map/all_to_all | solution.py:81
  99.7 3.1 %fusion.92 = (f32[128]{0:T(128)S(1)}, f32[128,1408]{1,0:T(8,128)S(1)}) fusion(bf16[2,4,176,1408]{3,2,1,0:T(8,128)(2,1)} %bitcast.12, bf16[4,2,128,176]{2,3,1,0:T(8,128)(2,1)S(1)} %bitcast.67, bf16[128,1408]{1,0:T(8,128)(2,1)S(1)} %copy-done.2), kind=kOutput, calls=%fused_computation.89 | convolution fusion | flops 508411776 | bytes 5407232 | tf_op jit(solution)/shard_map/xcqd,cxdo->qo/dot_general | solution.py:84
  102.7 0.2 multiply_reduce_fusion
  103.0 0.2 add_convert_fusion
  103.2 0.2 broadcast_in_dim.42
  103.5 1.2 broadcast_in_dim.78
  104.7 5.6 %all-to-all-start.3 = ((bf16[4,32,5632]{2,1,0:T(8,128)(2,1)}), bf16[4,32,5632]{2,1,0:T(8,128)(2,1)S(1)}, u32[]{:S(2)}, u32[]{:S(2)}) async-start(bf16[4,32,5632]{2,1,0:T(8,128)(2,1)} %broadcast_in_dim.78), calls=%async_computation.3 | async-start | bytes 2883584 | tf_op jit(solution)/shard_map/all_to_all | solution.py:89
  110.3 0.6 reduce-window.6
  110.9 0.2 slice_reduce_fusion
  111.1 0.1 fusion.68
  111.2 0.1 reduce_sum.66
  111.3 0.1 mul.59
  111.4 0.1 eq.86
  111.5 16.2 %all-to-all-done.3 = bf16[4,32,5632]{2,1,0:T(8,128)(2,1)S(1)} async-done(((bf16[4,32,5632]{2,1,0:T(8,128)(2,1)}), bf16[4,32,5632]{2,1,0:T(8,128)(2,1)S(1)}, u32[]{:S(2)}, u32[]{:S(2)}) %all-to-all-start.3) | async-done | bytes 1441824 | tf_op jit(solution)/shard_map/all_to_all | solution.py:89
  127.7 0.2 broadcast_in_dim.79
  127.9 7.0 %all_to_all.31 = bf16[2,4,32,5632]{3,2,1,0:T(8,128)(2,1)} all-to-all(bf16[2,4,32,5632]{3,2,1,0:T(8,128)(2,1)S(1)} %broadcast_in_dim.79), channel_id=1, replica_groups=mesh['y'=4,'z'=16,'x'=4,'core'=2] {'core'}, dimensions={0} | all-to-all | bytes 5767168 | tf_op jit(solution)/shard_map/all_to_all | solution.py:91
  134.9 15.8 %all-gather.7.cloned.1.call-done = bf16[4,1408,448]{2,1,0:T(8,128)(2,1)} async-done(((bf16[4,88,448]{2,1,0:T(8,128)(2,1)}), bf16[4,1408,448]{2,1,0:T(8,128)(2,1)}) %all-gather.7.cloned.1.call-update) | async-done | bytes 5046288 | tf_op jit(solution)/shard_map/all_gather | solution.py:64
  150.7 6.0 %convolution_convert_fusion = bf16[512,448]{0,1:T(8,128)(2,1)S(1)} fusion(bf16[256,5632]{1,0:T(8,128)(2,1)} %bitcast.61, bf16[5632,448]{1,0:T(8,128)(2,1)} %bitcast.71, s32[256]{0:T(256)S(1)} %eq.86, f32[448]{0:T(512)S(1)} %copy-done.11), kind=kOutput, calls=%fused_computation.36 | convolution fusion | flops 1409875968 | bytes 8391424 | tf_op jit(solution)/shard_map/dot_general | solution.py:107
  156.7 0.2 copy.22
  156.9 37.9 %all_to_all.32 = bf16[64,8,448]{2,1,0:T(8,128)(2,1)S(1)} all-to-all(bf16[64,8,448]{2,1,0:T(8,128)(2,1)S(1)} %bitcast.62), channel_id=1, replica_groups=mesh['y'=4,'z'=16,'x'=4,'core'=2] {'y','z'}, dimensions={0} | all-to-all | bytes 917504 | tf_op jit(solution)/shard_map/all_to_all | solution.py:111
  194.8 1.0 copy.23
  (41 shorter events, 0.3 us)
Async XLA Ops:
  6.5 64.8 %copy-start = (bf16[1408,2,264]{0,2,1:T(8,128)(2,1)S(1)}, bf16[1408,2,264]{0,2,1:T(8,128)(2,1)}, u32[]{:S(2)}) copy-start(bf16[1408,2,264]{0,2,1:T(8,128)(2,1)} %param.14) | copy-start | bytes 4460548
  6.5 25.0 %copy-start.8 = (s32[1,256]{1,0:T(1,128)S(1)}, s32[1,256]{1,0:T(1,128)}, u32[]{:S(2)}) copy-start(s32[1,256]{1,0:T(1,128)} %param.20) | copy-start | bytes 3076
  6.5 61.2 %all-gather.5.cloned.1.call-start = ((), (), s32[]{:S(2)}) async-start(), calls=%async_computation.6 | async-start | bytes 3244032 | tf_op jit(solution)/shard_map/all_gather | solution.py:65
  7.3 143.5 %all-gather.7.cloned.1.call-start = ((), (), s32[]{:S(2)}) async-start(), calls=%async_computation.7 | async-start | bytes 6127616 | tf_op jit(solution)/shard_map/all_gather | solution.py:64
  23.5 36.5 %all-to-all-start.1 = ((bf16[4,2,88,1408]{3,2,1,0:T(8,128)(2,1)}), bf16[4,2,88,1408]{3,2,1,0:T(8,128)(2,1)S(1)}, u32[]{:S(2)}, u32[]{:S(2)}) async-start(bf16[4,2,88,1408]{3,2,1,0:T(8,128)(2,1)} %broadcast_in_dim.40), calls=%async_computation.1 | async-start | bytes 3964928 | tf_op jit(solution)/shard_map/all_to_all | solution.py:68
  62.2 26.5 %all-to-all-start.2 = ((bf16[2,4,2,88,1408]{4,3,2,1,0:T(8,128)(2,1)}), bf16[2,4,2,88,1408]{4,3,2,1,0:T(8,128)(2,1)}, u32[]{:S(2)}, u32[]{:S(2)}) async-start(bf16[2,4,2,88,1408]{4,3,2,1,0:T(8,128)(2,1)} %broadcast_in_dim.41), calls=%async_computation.2 | async-start | bytes 7929856 | tf_op jit(solution)/shard_map/all_to_all | solution.py:69
  67.7 3.6 %copy-start.9 = (f32[1408]{0:T(1024)S(1)}, f32[1408]{0:T(1024)}, u32[]{:S(2)}) copy-start(f32[1408]{0:T(1024)} %param.13) | copy-start | bytes 16900
  67.7 2.7 %copy-start.1 = (bf16[1024,1408]{1,0:T(8,128)(2,1)S(1)}, bf16[1024,1408]{1,0:T(8,128)(2,1)}, u32[]{:S(2)}) copy-start(bf16[1024,1408]{1,0:T(8,128)(2,1)} %all-gather.5.cloned.1.call-done) | copy-start | bytes 8650756
  67.7 3.6 %copy-start.10 = (f32[1408]{0:T(1024)S(1)}, f32[1408]{0:T(1024)}, u32[]{:S(2)}) copy-start(f32[1408]{0:T(1024)} %param.12) | copy-start | bytes 16900
  71.3 3.2 %copy-start.4 = (pred[512,1024]{1,0:T(8,128)(4,1)S(1)}, pred[512,1024]{1,0:T(8,128)(4,1)}, u32[]{:S(2)}) copy-start(pred[512,1024]{1,0:T(8,128)(4,1)} %get-tuple-element.5) | copy-start | bytes 1572868
  74.5 4.8 %copy-start.3 = (pred[512,1024]{1,0:T(8,128)(4,1)S(1)}, pred[512,1024]{1,0:T(8,128)(4,1)}, u32[]{:S(2)}) copy-start(pred[512,1024]{1,0:T(8,128)(4,1)} %get-tuple-element.6) | copy-start | bytes 1572868
  79.3 4.9 %copy-start.12 = (bf16[1024,528]{0,1:T(8,128)(2,1)S(1)}, bf16[1024,528]{0,1:T(8,128)(2,1)}, u32[]{:S(2)}) copy-start(bf16[1024,528]{0,1:T(8,128)(2,1)} %fusion.27) | copy-start | bytes 3244036
  84.2 3.4 %copy-start.13 = (f32[2,512,1024]{2,1,0:T(8,128)S(1)}, f32[2,512,1024]{2,1,0:T(8,128)}, u32[]{:S(2)}) copy-start(f32[2,512,1024]{2,1,0:T(8,128)} %get-tuple-element.10) | copy-start | bytes 12582916
  87.6 12.1 %copy-start.2 = (bf16[128,1408]{1,0:T(8,128)(2,1)S(1)}, bf16[128,1408]{1,0:T(8,128)(2,1)}, u32[]{:S(2)}) copy-start(bf16[128,1408]{1,0:T(8,128)(2,1)} %param.11) | copy-start | bytes 1081348
  88.6 14.4 %copy-start.6 = (f32[1408]{0:T(1024)S(1)}, f32[1408]{0:T(1024)}, u32[]{:S(2)}) copy-start(f32[1408]{0:T(1024)} %param.17) | copy-start | bytes 16900
  88.6 14.4 %copy-start.7 = (f32[1408]{0:T(1024)S(1)}, f32[1408]{0:T(1024)}, u32[]{:S(2)}) copy-start(f32[1408]{0:T(1024)} %param.16) | copy-start | bytes 16900
  102.7 7.5 %copy-start.5 = (s32[256,1]{0,1:T(1,128)S(1)}, s32[256,1]{0,1:T(1,128)}, u32[]{:S(2)}) copy-start(s32[256,1]{0,1:T(1,128)} %param.21) | copy-start | bytes 3076
  104.7 23.0 %all-to-all-start.3 = ((bf16[4,32,5632]{2,1,0:T(8,128)(2,1)}), bf16[4,32,5632]{2,1,0:T(8,128)(2,1)S(1)}, u32[]{:S(2)}, u32[]{:S(2)}) async-start(bf16[4,32,5632]{2,1,0:T(8,128)(2,1)} %broadcast_in_dim.78), calls=%async_computation.3 | async-start | bytes 2883584 | tf_op jit(solution)/shard_map/all_to_all | solution.py:89
  127.9 22.8 %copy-start.11 = (f32[448]{0:T(512)S(1)}, f32[448]{0:T(512)}, u32[]{:S(2)}) copy-start(f32[448]{0:T(512)} %param.19) | copy-start | bytes 5380
Sparse Core Ops, SparseCore 0:
  9.5 47.0 all-gather.4
  58.7 91.9 all-gather.6

commit v9 on v7

--- a/solution.py
+++ b/solution.py
@@ -4,6 +4,7 @@
 from jax.sharding import Mesh, PartitionSpec as P
 
 DP = ("y", "z")
+IMAGE_TOKENS = 512
 TP = ("x", "core")
 
 
@@ -22,25 +23,29 @@
     keys_all = heads_qkv[:, :, width : 2 * width]
     values_all = heads_qkv[:, :, 2 * width :]
     score_scale = 1.0 / jnp.sqrt(jnp.float32(width))
-    block_rows = min(512, row_count)
+    block_rows = min(256, row_count)
     outputs = []
     for block_index in range(row_count // block_rows):
         lower = block_index * block_rows
+        key_lo = max(0, lower - IMAGE_TOKENS + 1) // 128 * 128
+        key_hi = min(row_count, -(-(lower + block_rows + IMAGE_TOKENS - 1) // 128) * 128)
         scores = (
             jnp.einsum(
                 "qhd,khd->hqk",
                 queries[lower : lower + block_rows],
-                keys_all,
+                keys_all[key_lo:key_hi],
                 preferred_element_type=jnp.float32,
             )
             * score_scale
         )
-        same = token_segs[lower : lower + block_rows][:, None] == token_segs[None, :]
+        same = token_segs[lower : lower + block_rows][:, None] == token_segs[None, key_lo:key_hi]
         scores = jnp.where(same[None], scores, -jnp.inf)
         row_max = jnp.max(scores, axis=-1, keepdims=True)
         exponent = jnp.exp(scores - row_max)
         probs = (exponent / jnp.sum(exponent, axis=-1, keepdims=True)).astype(jnp.bfloat16)
-        context = jnp.einsum("hqk,khd->qhd", probs, values_all, preferred_element_type=jnp.float32)
+        context = jnp.einsum(
+            "hqk,khd->qhd", probs, values_all[key_lo:key_hi], preferred_element_type=jnp.float32
+        )
         outputs.append(context.astype(jnp.bfloat16))
     return jnp.concatenate(outputs, axis=0)
 

time: 196 us -> 209 us (1.066)
  waiting for transfers between devices: 54 us -> 62.1 us
  local copies, waits for them, and re-layouts: 11 us -> 15.3 us
  matrix products: 25.4 us -> 23 us
    all_to_all x1, waiting for transfers between devices: 9.55 us -> 21.4 us  [shards(): lax.all_to_all(jnp.broadcast_to(w_out[None], (nx,) + w_out.shape), 'x', 0...]
    sub x2 -> x4, matrix products: 9.66 us -> 3.58 us  [attend(): exponent = jnp.exp(scores - row_max)]
    dot_general x2 -> x4, matrix products: 4.06 us -> 8.79 us  [attend(): jnp.einsum('hqk,khd->qhd', probs, values_all[key_lo:key_hi], preferred_el...]
    all_gather x1, waiting for transfers between devices: 8.98 us -> 5.25 us  [shards(): w_proj_all = lax.all_gather(w_y, 'z', axis=1).reshape(-1, w_proj.shape[1])]
    all_to_all x1, blocking collectives: 41 us -> 44.2 us  [shards(): lax.all_to_all(outgoing, DP, split_axis=0, concat_axis=0, tiled=True)]
    eq x3 -> x7, local copies, waits for them, and re-layouts: 1.26 us -> 3.46 us  [attend(): token_segs[lower:lower + block_rows][:, None]]
    all_to_all x1, blocking collectives: 13.1 us -> 11 us  [shards(): lax.all_to_all(context.reshape(tp_count, local_rows, -1), TP, 0, 0, tiled...]
  transfers between devices with their start and end apart: 5 -> 5, of which waited for: 4 -> 3; matrix products, arithmetic and copies ran while one was open for 18% -> 18% of each run, Pallas kernels for 0% -> 0%
where the time goes in v9:
time: 209 us; the launch traced here: 208 us
  blocking collectives  72.8 us (35%)
  waiting for transfers between devices  62.1 us (30%)
  matrix products  23 us (11%)
  local copies, waits for them, and re-layouts  15.3 us (7%)
  starting transfers between devices  14 us (7%)
  between operations  13.7 us (7%)
  other arithmetic  7.41 us (4%)
    all_to_all x1, blocking collectives, shards(): lax.all_to_all(outgoing, DP, split_axis=0, concat_axis=0, tiled=True)  44.2 us
    all_to_all x1, waiting for transfers between devices, shards(): lax.all_to_all(copies, TP, 0, 0, tiled=True)  34.6 us
    all_to_all x1, waiting for transfers between devices, shards(): lax.all_to_all(jnp.broadcast_to(w_out[None], (nx,) + w_out.shape), 'x', 0...  21.4 us
    all_gather x1, blocking collectives, shards(): w_y = lax.all_gather(w_proj, 'y', axis=0)  17.7 us
    all_to_all x1, blocking collectives, shards(): lax.all_to_all(context.reshape(tp_count, local_rows, -1), TP, 0, 0, tiled...  11 us
    dot_general x4, matrix products, attend(): jnp.einsum('hqk,khd->qhd', probs, values_all[key_lo:key_hi], preferred_el...  8.79 us
    all_to_all x1, starting transfers between devices, shards(): lax.all_to_all(jnp.broadcast_to(w_out_x[None], (nc,) + w_out_x.shape), 'c...  5.7 us
    dot_general x1, matrix products, shards(): jnp.dot(scatter_table, projected, preferred_element_type=jnp.float32)  5.46 us
  transfers between devices with their start and end apart: 5, of which 3 were waited for; matrix products, arithmetic and copies ran while one was open for 18% of the time, Pallas kernels for 0%

profile of v9, /device:TPU:8, one launch (start us, length us, event | category | flops | bytes accessed | tf_op | source)
XLA Modules:
  0.0 208.3 jit_solution(14719640565746177117)
XLA Ops:
  6.5 0.7 all-gather.5.cloned.1.call-update
  7.3 17.7 %all-gather = bf16[352,448]{1,0:T(8,128)(2,1)} all-gather(bf16[88,448]{1,0:T(8,128)(2,1)} %param.18), channel_id=2, replica_groups=mesh['y'=4,'z'=16,'x'=4,'core'=2] {'y'}, dimensions={0}, use_global_device_ids=true | all-gather | bytes 394240 | tf_op jit(solution)/shard_map/all_gather | solution.py:68
  25.0 2.5 %broadcast_in_dim.113 = bf16[4,2,88,1408]{3,2,1,0:T(8,128)(2,1)} broadcast(bf16[2,88,1408]{2,1,0:T(8,128)(2,1)} %param.15), dimensions={1,2,3} | broadcast | bytes 2478080 | tf_op jit(solution)/shard_map/broadcast_in_dim | solution.py:73
  27.5 3.8 %all-to-all-start.1 = ((bf16[4,2,88,1408]{3,2,1,0:T(8,128)(2,1)}), bf16[4,2,88,1408]{3,2,1,0:T(8,128)(2,1)S(1)}, u32[]{:S(2)}, u32[]{:S(2)}) async-start(bf16[4,2,88,1408]{3,2,1,0:T(8,128)(2,1)} %broadcast_in_dim.113), calls=%async_computation.1 | async-start | bytes 3964928 | tf_op jit(solution)/shard_map/all_to_all | solution.py:73
  31.4 0.1 eq.131
  31.6 0.1 eq.136
  31.7 0.8 broadcast_in_dim.105
  32.5 1.0 eq.133
  33.7 0.7 broadcast_in_dim.101
  34.5 1.0 eq.128
  35.7 0.7 broadcast_in_dim.111
  36.4 1.0 eq.141
  37.4 0.9 broadcast_compare_fusion.3
  38.2 0.9 broadcast_compare_fusion.2
  39.1 1.1 broadcast_compare_fusion.1
  40.2 21.4 %all-to-all-done.1 = bf16[4,2,88,1408]{3,2,1,0:T(8,128)(2,1)S(1)} async-done(((bf16[4,2,88,1408]{3,2,1,0:T(8,128)(2,1)}), bf16[4,2,88,1408]{3,2,1,0:T(8,128)(2,1)S(1)}, u32[]{:S(2)}, u32[]{:S(2)}) %all-to-all-start.1) | async-done | bytes 1982496 | tf_op jit(solution)/shard_map/all_to_all | solution.py:73
  61.7 2.3 %broadcast_in_dim.114 = bf16[2,4,2,88,1408]{4,3,2,1,0:T(8,128)(2,1)} broadcast(bf16[4,2,88,1408]{3,2,1,0:T(8,128)(2,1)S(1)} %all-to-all-done.1), dimensions={1,2,3,4} | broadcast | bytes 5947392 | tf_op jit(solution)/shard_map/broadcast_in_dim | solution.py:74
  63.9 5.7 %all-to-all-start.2 = ((bf16[2,4,2,88,1408]{4,3,2,1,0:T(8,128)(2,1)}), bf16[2,4,2,88,1408]{4,3,2,1,0:T(8,128)(2,1)}, u32[]{:S(2)}, u32[]{:S(2)}) async-start(bf16[2,4,2,88,1408]{4,3,2,1,0:T(8,128)(2,1)} %broadcast_in_dim.114), calls=%async_computation.2 | async-start | bytes 7929856 | tf_op jit(solution)/shard_map/all_to_all | solution.py:74
  69.7 2.4 %convert_reduce_fusion = f32[1024]{0:T(1024)S(1)} fusion(bf16[1024,1408]{1,0:T(8,128)(2,1)} %all-gather.5.cloned.1.call-done), kind=kLoop, calls=%fused_computation.5 | loop fusion | flops 2882560 | bytes 2887680 | tf_op jit(solution)/shard_map/reduce_sum | solution.py:13
  72.1 0.2 copy-done.1
  72.4 0.9 fusion.6
  73.3 2.1 %fusion.23 = bf16[1024,528]{0,1:T(8,128)(2,1)S(1)} fusion(bf16[1408,528]{0,1:T(8,128)(2,1)S(1)} %bitcast.68, bf16[1024,1408]{1,0:T(8,128)(2,1)S(1)} %copy-done.1, f32[1408]{0:T(1024)S(1)} %copy-done.11, f32[1408]{0:T(1024)S(1)} %copy-done.12, f32[1024]{0:T(1024)S(1)} %add_rsqrt_fusion, f32[1024]{0:T(1024)S(1)} %broadcast_multiply_fusion), kind=kOutput, calls=%fused_computation.35 | convolution fusion | flops 1531723776 | bytes 5471232 | tf_op jit(solution)/shard_map/dot_general | solution.py:78
  75.5 0.8 fusion.170
  76.3 0.3 copy-done.6
  76.6 0.8 fusion.155
  77.4 0.1 copy-done.4
  77.6 1.0 fusion.165
  78.6 1.0 fusion.160
  79.5 2.1 fusion.31
  81.6 2.1 fusion.32
  83.7 2.3 %fusion.29 = bf16[256,2,88]{0,2,1:T(8,128)(2,1)S(1)} fusion(f32[2,256]{1,0:T(2,128)S(1)} %fusion.165, bf16[1024,2,264]{0,2,1:T(8,128)(2,1)} %bitcast.88, pred[256,1024]{1,0:T(8,128)(4,1)S(1)} %copy-done.4), kind=kOutput, calls=%fused_computation.45 | convolution fusion | flops 187217408 | bytes 1165312 | tf_op jit(solution)/shard_map/hqk,khd->qhd/dot_general | solution.py:46
  86.0 2.3 %fusion.30 = bf16[256,2,88]{0,2,1:T(8,128)(2,1)S(1)} fusion(f32[2,256]{1,0:T(2,128)S(1)} %fusion.160, bf16[1024,2,264]{0,2,1:T(8,128)(2,1)} %bitcast.89, pred[256,1024]{1,0:T(8,128)(4,1)S(1)} %copy-done.3), kind=kOutput, calls=%fused_computation.46 | convolution fusion | flops 187217408 | bytes 1165312 | tf_op jit(solution)/shard_map/hqk,khd->qhd/dot_general | solution.py:46
  88.6 11.0 %all_to_all.25 = bf16[8,128,176]{1,2,0:T(8,128)(2,1)S(1)} all-to-all(bf16[8,128,176]{1,2,0:T(8,128)(2,1)S(1)} %copy.13), channel_id=1, replica_groups=mesh['y'=4,'z'=16,'x'=4,'core'=2] {'x','core'}, dimensions={0} | all-to-all | bytes 720896 | tf_op jit(solution)/shard_map/all_to_all | solution.py:86
  99.5 3.1 %fusion.175 = (f32[128]{0:T(128)S(1)}, f32[128,1408]{1,0:T(8,128)S(1)}) fusion(bf16[2,4,176,1408]{3,2,1,0:T(8,128)(2,1)} %bitcast.17, bf16[4,2,128,176]{2,3,1,0:T(8,128)(2,1)S(1)} %bitcast.74, bf16[128,1408]{1,0:T(8,128)(2,1)S(1)} %copy-done.2), kind=kOutput, calls=%fused_computation.125 | convolution fusion | flops 508411776 | bytes 5407232 | tf_op jit(solution)/shard_map/xcqd,cxdo->qo/dot_general | solution.py:89
  102.6 0.2 multiply_reduce_fusion
  102.9 0.2 add_convert_fusion
  103.1 0.2 broadcast_in_dim.115
  103.4 1.9 broadcast_in_dim.116
  105.3 4.6 %all-to-all-start.3 = ((bf16[8,32,5632]{2,1,0:T(8,128)(2,1)}), bf16[8,32,5632]{2,1,0:T(8,128)(2,1)}, u32[]{:S(2)}, u32[]{:S(2)}) async-start(bf16[8,32,5632]{2,1,0:T(8,128)(2,1)} %broadcast_in_dim.116), calls=%async_computation.3 | async-start | bytes 5767168 | tf_op jit(solution)/shard_map/all_to_all | solution.py:94
  109.8 0.6 reduce-window.6
  110.4 0.2 slice_reduce_fusion
  110.7 0.1 fusion.96
  110.8 34.6 %all-to-all-done.3 = bf16[8,32,5632]{2,1,0:T(8,128)(2,1)} async-done(((bf16[8,32,5632]{2,1,0:T(8,128)(2,1)}), bf16[8,32,5632]{2,1,0:T(8,128)(2,1)}, u32[]{:S(2)}, u32[]{:S(2)}) %all-to-all-start.3) | async-done | bytes 2883616 | tf_op jit(solution)/shard_map/all_to_all | solution.py:94
  145.4 5.2 %all-gather.7.cloned.1.call-done = bf16[4,1408,448]{2,1,0:T(8,128)(2,1)} async-done(((bf16[4,88,448]{2,1,0:T(8,128)(2,1)}), bf16[4,1408,448]{2,1,0:T(8,128)(2,1)}) %all-gather.7.cloned.1.call-update) | async-done | bytes 5046288 | tf_op jit(solution)/shard_map/all_gather | solution.py:69
  150.7 5.5 %convolution_convert_fusion = bf16[512,448]{0,1:T(8,128)(2,1)S(1)} fusion(bf16[256,5632]{1,0:T(8,128)(2,1)} %bitcast.20, bf16[5632,448]{1,0:T(8,128)(2,1)} %bitcast.81, f32[448]{0:T(512)S(1)} %copy-done.13, s32[256]{0:T(256)S(1)} %multiply_add_fusion), kind=kOutput, calls=%fused_computation.38 | convolution fusion | flops 1409875968 | bytes 8391424 | tf_op jit(solution)/shard_map/dot_general | solution.py:109
  156.2 0.2 copy.15
  156.4 44.2 %all_to_all.26 = bf16[64,8,448]{2,1,0:T(8,128)(2,1)S(1)} all-to-all(bf16[64,8,448]{2,1,0:T(8,128)(2,1)S(1)} %bitcast.69), channel_id=1, replica_groups=mesh['y'=4,'z'=16,'x'=4,'core'=2] {'y','z'}, dimensions={0} | all-to-all | bytes 917504 | tf_op jit(solution)/shard_map/all_to_all | solution.py:113
  200.5 1.0 copy.16
  (51 shorter events, 1.0 us)
Async XLA Ops:
  6.5 66.7 %copy-start = (bf16[1408,2,264]{0,2,1:T(8,128)(2,1)S(1)}, bf16[1408,2,264]{0,2,1:T(8,128)(2,1)}, u32[]{:S(2)}) copy-start(bf16[1408,2,264]{0,2,1:T(8,128)(2,1)} %param.14) | copy-start | bytes 4460548
  6.5 63.1 %all-gather.5.cloned.1.call-start = ((), (), s32[]{:S(2)}) async-start(), calls=%async_computation.5 | async-start | bytes 3244032 | tf_op jit(solution)/shard_map/all_gather | solution.py:70
  7.3 143.4 %all-gather.7.cloned.1.call-start = ((), (), s32[]{:S(2)}) async-start(), calls=%async_computation.6 | async-start | bytes 6127616 | tf_op jit(solution)/shard_map/all_gather | solution.py:69
  27.5 3.8 %copy-start.7 = (s32[1,256]{1,0:T(1,128)S(1)}, s32[1,256]{1,0:T(1,128)}, u32[]{:S(2)}) copy-start(s32[1,256]{1,0:T(1,128)} %param.20) | copy-start | bytes 3076
  27.5 34.2 %all-to-all-start.1 = ((bf16[4,2,88,1408]{3,2,1,0:T(8,128)(2,1)}), bf16[4,2,88,1408]{3,2,1,0:T(8,128)(2,1)S(1)}, u32[]{:S(2)}, u32[]{:S(2)}) async-start(bf16[4,2,88,1408]{3,2,1,0:T(8,128)(2,1)} %broadcast_in_dim.113), calls=%async_computation.1 | async-start | bytes 3964928 | tf_op jit(solution)/shard_map/all_to_all | solution.py:73
  63.9 24.6 %all-to-all-start.2 = ((bf16[2,4,2,88,1408]{4,3,2,1,0:T(8,128)(2,1)}), bf16[2,4,2,88,1408]{4,3,2,1,0:T(8,128)(2,1)}, u32[]{:S(2)}, u32[]{:S(2)}) async-start(bf16[2,4,2,88,1408]{4,3,2,1,0:T(8,128)(2,1)} %broadcast_in_dim.114), calls=%async_computation.2 | async-start | bytes 7929856 | tf_op jit(solution)/shard_map/all_to_all | solution.py:74
  69.7 2.7 %copy-start.1 = (bf16[1024,1408]{1,0:T(8,128)(2,1)S(1)}, bf16[1024,1408]{1,0:T(8,128)(2,1)}, u32[]{:S(2)}) copy-start(bf16[1024,1408]{1,0:T(8,128)(2,1)} %all-gather.5.cloned.1.call-done) | copy-start | bytes 8650756
  72.1 1.2 copy-start.11
  72.1 1.2 copy-start.12
  73.3 2.1 %copy-start.5 = (pred[256,768]{1,0:T(8,128)(4,1)S(1)}, pred[256,768]{1,0:T(8,128)(4,1)}, u32[]{:S(2)}) copy-start(pred[256,768]{1,0:T(8,128)(4,1)} %broadcast_compare_fusion.3) | copy-start | bytes 589828
  75.4 3.1 %copy-start.14 = (bf16[1024,528]{0,1:T(8,128)(2,1)}, bf16[1024,528]{0,1:T(8,128)(2,1)S(1)}, u32[]{:S(2)}) copy-start(bf16[1024,528]{0,1:T(8,128)(2,1)S(1)} %fusion.23) | copy-start | bytes 3244036
  75.4 1.2 copy-start.6
  76.6 0.9 copy-start.4
  77.6 1.0 copy-start.3
  88.4 11.2 %copy-start.2 = (bf16[128,1408]{1,0:T(8,128)(2,1)S(1)}, bf16[128,1408]{1,0:T(8,128)(2,1)}, u32[]{:S(2)}) copy-start(bf16[128,1408]{1,0:T(8,128)(2,1)} %param.11) | copy-start | bytes 1081348
  99.5 3.4 %copy-start.9 = (f32[1408]{0:T(1024)S(1)}, f32[1408]{0:T(1024)}, u32[]{:S(2)}) copy-start(f32[1408]{0:T(1024)} %param.17) | copy-start | bytes 16900
  99.5 3.4 %copy-start.10 = (f32[1408]{0:T(1024)S(1)}, f32[1408]{0:T(1024)}, u32[]{:S(2)}) copy-start(f32[1408]{0:T(1024)} %param.16) | copy-start | bytes 16900
  105.2 4.6 %copy-start.8 = (s32[256,1]{0,1:T(1,128)S(1)}, s32[256,1]{0,1:T(1,128)}, u32[]{:S(2)}) copy-start(s32[256,1]{0,1:T(1,128)} %param.21) | copy-start | bytes 3076
  105.2 45.4 %copy-start.13 = (f32[448]{0:T(512)S(1)}, f32[448]{0:T(512)}, u32[]{:S(2)}) copy-start(f32[448]{0:T(512)} %param.19) | copy-start | bytes 5380
  105.3 40.2 %all-to-all-start.3 = ((bf16[8,32,5632]{2,1,0:T(8,128)(2,1)}), bf16[8,32,5632]{2,1,0:T(8,128)(2,1)}, u32[]{:S(2)}, u32[]{:S(2)}) async-start(bf16[8,32,5632]{2,1,0:T(8,128)(2,1)} %broadcast_in_dim.116), calls=%async_computation.3 | async-start | bytes 5767168 | tf_op jit(solution)/shard_map/all_to_all | solution.py:94
Sparse Core Ops, SparseCore 0:
  9.5 48.6 all-gather.4
  60.3 90.3 all-gather.6
